TPU v7x, 512 devices: a whole 4x8x8 slice. The times are simulated.
512 devices in a mesh: fsdp: 8 (over z_hi, core), seq: 64 (over z_lo, x, y).
Axes of the slice: x: 4, y: 8, z: 8 (z_hi: 4, z_lo: 2; z = z_hi * 2 + z_lo), core: 2. Of those that a mesh axis runs over, the one named last changes fastest.
Arguments:
- hidden: bfloat16 [8192, 8192], P('seq', 'fsdp'), may hold values from -6 to 6
- queries: bfloat16 [8192, 8192], P('seq', 'fsdp'), may hold values from -160 to 160
- kv_weight: bfloat16 [8192, 2048], P('fsdp'), may hold values from -0.09375 to 0.09375
- kv_bias: float32 [2048], replicated, may hold values from -5 to 5
- parents: int32 [64], replicated, may hold values from 0 to 62, as said below
- slot_block: int32 [64], replicated, may hold values from 0 to 63, each once
Outputs:
- attended: bfloat16 [8192, 8192], P('seq', 'fsdp')
Inputs may be any that keep to these rules, and one draw needn't show every extreme that they name: parents[0] = 0; every other block's parent has a lower number; blocks below 32 form one chain from block 0.
All inputs are finite; a program needn't handle non-finite values.
Results may differ from a plain program's by a relative error of at most 0.018.
Values may be sent and summed in bfloat16 or wider, within the bound.
No kernel may reach another device: no remote copies, remote signals or barrier semaphores. Data moves between devices by JAX's collectives and lax.ppermute only.
A program may use at most 64 MiB of HBM per device.

v0:
```python
import math

import jax
import jax.numpy as jnp
from jax import lax
from jax.sharding import PartitionSpec as P

HD = 128
BLOCK = 128


def ancestry_table(parents, slot_block):
    block_count = parents.shape[0]
    block_ids = jnp.arange(block_count, dtype=jnp.int32)
    linked = (parents[:, None] == block_ids[None, :]).astype(jnp.float32)
    ancestry = jnp.maximum(jnp.eye(block_count, dtype=jnp.float32), linked)
    for sweep in range(block_count.bit_length()):
        ancestry = jnp.minimum(jnp.dot(ancestry, ancestry, precision=lax.Precision.HIGHEST), 1.0)
    placement = (slot_block[:, None] == block_ids[None, :]).astype(jnp.float32)
    first_pass = jnp.dot(placement, ancestry, precision=lax.Precision.HIGHEST)
    return jnp.dot(first_pass, placement.T, precision=lax.Precision.HIGHEST)


def keep_state(state_now):
    return state_now


def shards(hidden, queries, kv_weight, kv_bias, parents, slot_block):
    tok_rows = hidden.shape[0]
    per_device = tok_rows // BLOCK
    head_count = queries.shape[1] // HD
    score_scale = 1.0 / math.sqrt(HD)
    fsdp_index = lax.axis_index("fsdp")
    partial_sums = jnp.dot(hidden, kv_weight, preferred_element_type=jnp.float32)
    head_bias = lax.dynamic_slice_in_dim(kv_bias, fsdp_index * 2 * HD, 2 * HD, 0)
    summed = lax.psum(partial_sums, "fsdp")
    head_cols = lax.dynamic_slice_in_dim(summed, fsdp_index * 2 * HD, 2 * HD, 1)
    both_parts = (head_cols + head_bias).astype(jnp.bfloat16)
    key_rows = both_parts[:, :HD]
    value_rows = both_parts[:, HD:]
    visible = ancestry_table(parents, slot_block)
    first_slot = lax.axis_index("seq") * per_device
    own_visible = lax.dynamic_slice_in_dim(visible, first_slot, per_device, 0)
    row_slot = first_slot + jnp.arange(tok_rows, dtype=jnp.int32) // BLOCK
    row_offset = jnp.arange(tok_rows, dtype=jnp.int32) % BLOCK
    query_heads = queries.reshape(tok_rows, head_count, HD)
    initial = (
        jnp.full((tok_rows, head_count), -1e30, jnp.float32),
        jnp.zeros((tok_rows, head_count), jnp.float32),
        jnp.zeros((tok_rows, head_count, HD), jnp.float32),
    )
    key_piece = lax.all_gather(key_rows, "seq", axis=0, tiled=True)
    value_piece = lax.all_gather(value_rows, "seq", axis=0, tiled=True)
    piece_blocks = key_piece.shape[0] // BLOCK
    group = math.gcd(piece_blocks, 8)
    tile = group * BLOCK
    tile_count = piece_blocks // group
    key_offset = jnp.arange(tile, dtype=jnp.int32) % BLOCK
    key_inner = jnp.arange(tile, dtype=jnp.int32) // BLOCK

    def one_tile(tile_index, state_now):
        key_slot_first = tile_index * group
        tile_visible = lax.dynamic_slice_in_dim(own_visible, key_slot_first, group, 1)

        def attend(state_in):
            running_max, running_sum, numerator = state_in
            key_tile = lax.dynamic_slice_in_dim(key_piece, tile_index * tile, tile, 0)
            value_tile = lax.dynamic_slice_in_dim(value_piece, tile_index * tile, tile, 0)
            scores = (
                jnp.einsum("qhd,kd->qhk", query_heads, key_tile, preferred_element_type=jnp.float32)
                * score_scale
            )
            spread = jnp.repeat(jnp.repeat(tile_visible, BLOCK, axis=0), BLOCK, axis=1) > 0.5
            key_slot = key_slot_first + key_inner
            allowed = spread & (
                (row_slot[:, None] != key_slot[None, :])
                | (key_offset[None, :] <= row_offset[:, None])
            )
            masked = jnp.where(allowed[:, None, :], scores, -1e30)
            new_max = jnp.maximum(running_max, jnp.max(masked, axis=-1))
            expo = jnp.where(allowed[:, None, :], jnp.exp(masked - new_max[..., None]), 0.0)
            factor = jnp.exp(running_max - new_max)
            new_sum = running_sum * factor + jnp.sum(expo, axis=-1)
            update = jnp.einsum(
                "qhk,kd->qhd",
                expo.astype(jnp.bfloat16),
                value_tile,
                preferred_element_type=jnp.float32,
            )
            new_numerator = numerator * factor[..., None] + update
            return (new_max, new_sum, new_numerator)

        return lax.cond(jnp.max(tile_visible) > 0.5, attend, keep_state, state_now)

    final_max, final_sum, final_numerator = lax.fori_loop(0, tile_count, one_tile, initial)
    attended = final_numerator / final_sum[..., None]
    return attended.reshape(tok_rows, head_count * HD).astype(jnp.bfloat16)


def solution(mesh):
    return jax.shard_map(
        shards,
        mesh=mesh,
        in_specs=(P("seq", "fsdp"), P("seq", "fsdp"), P("fsdp", None), P(), P(), P()),
        out_specs=P("seq", "fsdp"),
        check_vma=False,
    )
```

profile of v0, /device:TPU:6, one launch (start us, length us, event | category | flops | bytes accessed | tf_op | source)
XLA Modules:
  0.0 760.7 jit_solution(17489612144787789115)
XLA Ops:
  7.5 3.9 fusion.43
  12.2 87.0 %all-reduce.2.cloned.1.call-done = f32[128,2048]{1,0:T(8,128)} async-done(((f32[128,2048]{1,0:T(8,128)}), f32[128,2048]{1,0:T(8,128)}) %all-reduce.2.cloned.1.call-update) | async-done | bytes 1048592 | tf_op jit(solution)/shard_map/psum | solution.py:36
  103.7 286.3 %all-gather.3.cloned.1.call-done = bf16[8192,128]{1,0:T(8,128)(2,1)} async-done(((bf16[128,128]{1,0:T(8,128)(2,1)}), bf16[8192,128]{1,0:T(8,128)(2,1)}) %all-gather.3.cloned.1.call-update) | async-done | bytes 2097168 | tf_op jit(solution)/shard_map/all_gather | solution.py:52
  390.0 301.9 %all-gather.5.cloned.1.call-done = bf16[8192,128]{1,0:T(8,128)(2,1)} async-done(((bf16[128,128]{1,0:T(8,128)(2,1)}), bf16[8192,128]{1,0:T(8,128)(2,1)}) %all-gather.5.cloned.1.call-update) | async-done | bytes 2097168 | tf_op jit(solution)/shard_map/all_gather | solution.py:53
  691.9 61.3 %while.18 = (s32[]{:T(128)}, f32[128,8]{0,1:T(8,128)S(1)}, f32[128,8]{0,1:T(8,128)S(1)}, f32[128,8,128]{2,0,1:T(8,128)S(1)}, f32[1,64]{1,0:T(1,128)S(1)}, /*inde...) while((s32[]{:T(128)}, f32[128,8]{0,1:T(8,128)S(1)}, ...), condition=%wide.region_7.8_spmd.clone, body=%wide.region_1.7_spmd.clone.sunk | while | flops 551307008 | bytes 15081951 | solution.py:95
  693.4 6.2 conditional.3
  694.4 1.7 fusion.8
  696.1 1.0 fusion.10
  697.2 2.4 fusion.14
  701.1 6.2 conditional.3
  702.1 1.7 fusion.8
  703.8 1.0 fusion.10
  704.8 2.4 fusion.14
  708.7 6.2 conditional.3
  709.7 1.7 fusion.8
  711.5 1.0 fusion.10
  712.5 2.4 fusion.14
  716.4 6.2 conditional.3
  717.4 1.7 fusion.8
  720.2 2.4 fusion.14
  724.1 6.2 conditional.3
  725.1 1.7 fusion.8
  727.8 2.4 fusion.14
  731.7 6.2 conditional.3
  732.7 1.7 fusion.8
  735.5 2.4 fusion.14
  739.4 6.2 conditional.3
  740.4 1.7 fusion.8
  743.1 2.4 fusion.14
  747.0 6.2 conditional.3
  748.0 1.7 fusion.8
  750.8 2.4 fusion.14
  (174 shorter events, 25.9 us)
Async XLA Ops:
  6.5 1.0 copy-start
  6.5 95.0 %copy-start.1 = (bf16[128,1024]{1,0:T(8,128)(2,1)S(1)}, bf16[128,1024]{1,0:T(8,128)(2,1)}, u32[]{:S(2)}) copy-start(bf16[128,1024]{1,0:T(8,128)(2,1)} %param.11) | copy-start | bytes 786436
  6.5 95.4 %copy-start.3 = (s32[64]{0:T(128)S(1)}, s32[64]{0:T(128)}, u32[]{:S(2)}) copy-start(s32[64]{0:T(128)} %param.14) | copy-start | bytes 772
  6.5 96.7 %copy-start.2 = (s32[64]{0:T(128)S(1)}, s32[64]{0:T(128)}, u32[]{:S(2)}) copy-start(s32[64]{0:T(128)} %param.15) | copy-start | bytes 772
  6.5 92.7 %all-reduce.2.cloned.1.call-start = ((), (), s32[]{:S(2)}) async-start(), calls=%async_computation | async-start | bytes 2097152 | tf_op jit(solution)/shard_map/psum | solution.py:36
  11.4 378.6 %all-gather.3.cloned.1.call-start = ((), (), s32[]{:S(2)}) async-start(), calls=%async_computation.1 | async-start | bytes 2129920 | tf_op jit(solution)/shard_map/all_gather | solution.py:52
  100.8 591.0 %all-gather.5.cloned.1.call-start = ((), (), s32[]{:S(2)}) async-start(), calls=%async_computation.2 | async-start | bytes 2129920 | tf_op jit(solution)/shard_map/all_gather | solution.py:53
Sparse Core Ops, SparseCore 0:
  11.5 87.6 all-reduce.1
  101.3 288.5 all-gather.2
  392.1 299.7 all-gather.4
where the time goes:
time: 773 us; the launch traced here: 761 us
  waiting for transfers between devices  676 us (87%)
  matrix products  38.3 us (5%)
  other arithmetic  23 us (3%)
  between operations  13.3 us (2%)
    all_gather x1, waiting for transfers between devices, shards(): value_piece = lax.all_gather(value_rows, 'seq', axis=0, tiled=True)  302 us
    all_gather x1, waiting for transfers between devices, shards(): key_piece = lax.all_gather(key_rows, 'seq', axis=0, tiled=True)  286 us
    psum x1, waiting for transfers between devices, shards(): summed = lax.psum(partial_sums, 'fsdp')  87 us
    dot_general x8, matrix products, attend(): jnp.einsum('qhk,kd->qhd', expo.astype(jnp.bfloat16), value_tile, preferre...  19.1 us
  transfers between devices with their start and end apart: 3, of which 3 were waited for; matrix products, arithmetic and copies ran while one was open for 0% of the time, Pallas kernels for 0%

commit v1 on v0

--- a/solution.py
+++ b/solution.py
@@ -2,11 +2,15 @@
 
 import jax
 import jax.numpy as jnp
+import numpy as np
 from jax import lax
+from jax.sharding import Mesh
 from jax.sharding import PartitionSpec as P
 
 HD = 128
 BLOCK = 128
+FSDP_AXES = ("zh", "c")
+SEQ_AXES = ("zl", "x", "y")
 
 
 def ancestry_table(parents, slot_block):
@@ -25,21 +29,32 @@
     return state_now
 
 
+def seq_index():
+    return (lax.axis_index("zl") * lax.axis_size("x") + lax.axis_index("x")) * lax.axis_size("y") + lax.axis_index("y")
+
+
+def fsdp_index():
+    return lax.axis_index("zh") * lax.axis_size("c") + lax.axis_index("c")
+
+
 def shards(hidden, queries, kv_weight, kv_bias, parents, slot_block):
     tok_rows = hidden.shape[0]
     per_device = tok_rows // BLOCK
     head_count = queries.shape[1] // HD
     score_scale = 1.0 / math.sqrt(HD)
-    fsdp_index = lax.axis_index("fsdp")
+    f_index = fsdp_index()
+    n_zh = lax.axis_size("zh")
+    n_c = lax.axis_size("c")
     partial_sums = jnp.dot(hidden, kv_weight, preferred_element_type=jnp.float32)
-    head_bias = lax.dynamic_slice_in_dim(kv_bias, fsdp_index * 2 * HD, 2 * HD, 0)
-    summed = lax.psum(partial_sums, "fsdp")
-    head_cols = lax.dynamic_slice_in_dim(summed, fsdp_index * 2 * HD, 2 * HD, 1)
+    cols = partial_sums.shape[1]
+    per_head = cols // (n_zh * n_c)
+    regrouped = partial_sums.reshape(tok_rows, n_zh, n_c, per_head).transpose(0, 2, 1, 3).reshape(tok_rows, cols)
+    half = lax.psum_scatter(regrouped, "c", scatter_dimension=1, tiled=True)
+    head_cols = lax.psum_scatter(half, "zh", scatter_dimension=1, tiled=True)
+    head_bias = lax.dynamic_slice_in_dim(kv_bias, f_index * 2 * HD, 2 * HD, 0)
     both_parts = (head_cols + head_bias).astype(jnp.bfloat16)
-    key_rows = both_parts[:, :HD]
-    value_rows = both_parts[:, HD:]
     visible = ancestry_table(parents, slot_block)
-    first_slot = lax.axis_index("seq") * per_device
+    first_slot = seq_index() * per_device
     own_visible = lax.dynamic_slice_in_dim(visible, first_slot, per_device, 0)
     row_slot = first_slot + jnp.arange(tok_rows, dtype=jnp.int32) // BLOCK
     row_offset = jnp.arange(tok_rows, dtype=jnp.int32) % BLOCK
@@ -49,8 +64,13 @@
         jnp.zeros((tok_rows, head_count), jnp.float32),
         jnp.zeros((tok_rows, head_count, HD), jnp.float32),
     )
-    key_piece = lax.all_gather(key_rows, "seq", axis=0, tiled=True)
-    value_piece = lax.all_gather(value_rows, "seq", axis=0, tiled=True)
+    gathered = lax.all_gather(both_parts, "zl", axis=0, tiled=True)
+    gathered = lax.all_gather(gathered, "y", axis=0, tiled=True)
+    gathered = lax.all_gather(gathered, "x", axis=0, tiled=True)
+    n_zl, n_x, n_y = lax.axis_size("zl"), lax.axis_size("x"), lax.axis_size("y")
+    gathered = gathered.reshape(n_x, n_y, n_zl, tok_rows, 2 * HD).transpose(2, 0, 1, 3, 4).reshape(-1, 2 * HD)
+    key_piece = gathered[:, :HD]
+    value_piece = gathered[:, HD:]
     piece_blocks = key_piece.shape[0] // BLOCK
     group = math.gcd(piece_blocks, 8)
     tile = group * BLOCK
@@ -98,10 +118,18 @@
 
 
 def solution(mesh):
+    n_fsdp, n_seq = mesh.devices.shape
+    n_c = 2
+    n_zh = n_fsdp // n_c
+    n_zl = 2
+    n_y = 8
+    n_x = n_seq // (n_zl * n_y)
+    fine = Mesh(mesh.devices.reshape(n_zh, n_c, n_zl, n_x, n_y), FSDP_AXES + SEQ_AXES)
+    tok = P(SEQ_AXES, FSDP_AXES)
     return jax.shard_map(
         shards,
-        mesh=mesh,
-        in_specs=(P("seq", "fsdp"), P("seq", "fsdp"), P("fsdp", None), P(), P(), P()),
-        out_specs=P("seq", "fsdp"),
+        mesh=fine,
+        in_specs=(tok, tok, P(FSDP_AXES, None), P(), P(), P()),
+        out_specs=tok,
         check_vma=False,
     )

time: 773 us -> 243 us (0.31); the launches traced: 761 us -> 240 us
  waiting for transfers between devices: 676 us -> 147 us
  local copies, waits for them, and re-layouts: 3.39 us -> 15.5 us
  matrix products: 38.3 us -> 29.6 us
    all_gather x2, waiting for transfers between devices: 588 us -> 91.6 us  [the longest x1 51 us: shards(): gathered = lax.all_gather(gathered, 'x', axis=0, tiled=True)]
    psum x1 -> x0, waiting for transfers between devices: 87 us -> none  [shards(): summed = lax.psum(partial_sums, 'fsdp')]
    reduce_scatter x0 -> x2, waiting for transfers between devices: none -> 55.5 us  [the longest x1 34.2 us: shards(): head_cols = lax.psum_scatter(half, 'zh', scatter_dimension=1, tiled=True)]
  transfers between devices with their start and end apart: 3 -> 4, of which waited for: 3 -> 4; matrix products, arithmetic and copies ran while one was open for 0% -> 1% of each run, Pallas kernels for 0% -> 0%
where the time goes in v1:
time: 243 us; the launch traced here: 240 us
  waiting for transfers between devices  147 us (60%)
  matrix products  29.6 us (12%)
  other arithmetic  22.8 us (9%)
  local copies, waits for them, and re-layouts  15.5 us (6%)
  between operations  13.3 us (5%)
  loops' own time  6.09 us (3%)
  blocking collectives  5.07 us (2%)
    all_gather x1, waiting for transfers between devices, shards(): gathered = lax.all_gather(gathered, 'x', axis=0, tiled=True)  51 us
    all_gather x1, waiting for transfers between devices, shards(): gathered = lax.all_gather(gathered, 'y', axis=0, tiled=True)  40.6 us
    reduce_scatter x1, waiting for transfers between devices, shards(): head_cols = lax.psum_scatter(half, 'zh', scatter_dimension=1, tiled=True)  34.2 us
    reduce_scatter x1, waiting for transfers between devices, shards(): half = lax.psum_scatter(regrouped, 'c', scatter_dimension=1, tiled=True)  21.3 us
    dot_general x8, matrix products, attend(): jnp.einsum('qhk,kd->qhd', expo.astype(jnp.bfloat16), value_tile, preferre...  19.1 us
    reduce_sum x8, other arithmetic, attend(): new_sum = running_sum * factor + jnp.sum(expo, axis=-1)  8.05 us
    and x8, other arithmetic, attend(): spread & ((row_slot[:, None] != key_slot[None, :]) | (key_offset[None, :]...  6.74 us
    all_gather x1, local copies, waits for them, and re-layouts, shards(): gathered = lax.all_gather(gathered, 'x', axis=0, tiled=True)  6.42 us
  transfers between devices with their start and end apart: 4, of which 4 were waited for; matrix products, arithmetic and copies ran while one was open for 1% of the time, Pallas kernels for 0%

profile of v1, /device:TPU:6, one launch (start us, length us, event | category | flops | bytes accessed | tf_op | source)
XLA Modules:
  0.0 239.7 jit_solution(8442489414908024766)
XLA Ops:
  7.5 2.9 %fusion.43 = f32[128,2048]{1,0:T(8,128)S(1)} fusion(bf16[128,1024]{1,0:T(8,128)(2,1)S(1)} %copy-done, bf16[1024,2048]{1,0:T(8,128)(2,1)} %param.12), kind=kOutput, calls=%fused_computation.70 | convolution fusion | flops 536870912 | bytes 5505024 | tf_op jit(solution)/shard_map/dot_general | solution.py:48
  11.3 1.3 copy.16
  12.7 21.3 %reduce-scatter.3.cloned.1.call-done = f32[128,1024]{0,1:T(8,128)} async-done(((f32[128,2048]{0,1:T(8,128)}), f32[128,1024]{0,1:T(8,128)}) %reduce-scatter.3.cloned.1.call-update) | async-done | bytes 524304 | tf_op jit(solution)/shard_map/reduce_scatter | solution.py:52
  34.8 34.2 %reduce-scatter.5.cloned.1.call-done = f32[128,256]{0,1:T(8,128)} async-done(((f32[128,1024]{0,1:T(8,128)}), f32[128,256]{0,1:T(8,128)}) %reduce-scatter.5.cloned.1.call-update) | async-done | bytes 131088 | tf_op jit(solution)/shard_map/reduce_scatter | solution.py:53
  70.1 5.1 %all_gather.9 = bf16[256,256]{0,1:T(8,128)(2,1)} all-gather(bf16[128,256]{0,1:T(8,128)(2,1)S(1)} %add_convert_fusion), channel_id=1, replica_groups=mesh['zh'=4,'c'=2,'zl'=2,'x'=4,'y'=8] {'zl'}, dimensions={0}, use_global_device_ids=true | all-gather | bytes 196608 | tf_op jit(solution)/shard_map/all_gather | solution.py:67
  75.2 40.6 %all-gather.3.cloned.1.call-done = bf16[2048,256]{0,1:T(8,128)(2,1)} async-done(((bf16[256,256]{0,1:T(8,128)(2,1)}), bf16[2048,256]{0,1:T(8,128)(2,1)}) %all-gather.3.cloned.1.call-update) | async-done | bytes 1048592 | tf_op jit(solution)/shard_map/all_gather | solution.py:68
  118.0 51.0 %all-gather.5.cloned.1.call-done = bf16[8192,256]{0,1:T(8,128)(2,1)} async-done(((bf16[2048,256]{0,1:T(8,128)(2,1)}), bf16[8192,256]{0,1:T(8,128)(2,1)}) %all-gather.5.cloned.1.call-update) | async-done | bytes 4194320 | tf_op jit(solution)/shard_map/all_gather | solution.py:69
  169.0 6.4 %copy.17 = bf16[8192,256]{1,0:T(8,128)(2,1)} copy(bf16[8192,256]{0,1:T(8,128)(2,1)} %all-gather.5.cloned.1.call-done) | data formatting | bytes 8388608 | tf_op jit(solution)/shard_map/all_gather | solution.py:69
  175.4 2.5 %copy.18 = bf16[2,4,8,128,256]{4,3,2,1,0:T(8,128)(2,1)S(1)} copy(bf16[2,4,8,128,256]{4,3,0,2,1:T(8,128)(2,1)} %bitcast.61) | data formatting | bytes 8388608 | tf_op jit(solution)/shard_map/transpose | solution.py:71
  177.9 1.6 fusion.42
  179.5 52.8 %while.18 = (s32[]{:T(128)}, f32[128,8]{0,1:T(8,128)S(1)}, f32[128,8]{0,1:T(8,128)S(1)}, f32[128,8,128]{2,0,1:T(8,128)S(1)}, f32[1,64]{1,0:T(1,128)S(1)}, /*inde...) while((s32[]{:T(128)}, f32[128,8]{0,1:T(8,128)S(1)}, ...), condition=%wide.region_8.9_spmd.clone, body=%wide.region_2.8_spmd.clone.sunk | while | flops 551307008 | bytes 15081951 | solution.py:115
  180.9 5.2 %conditional.3 = ((f32[128,8]{0,1:T(8,128)S(1)}, f32[128,8]{0,1:T(8,128)S(1)}, f32[128,8,128]{2,0,1:T(8,128)S(1)})) conditional(s32[]{:T(128)} %convert_element_type.51, (f32[128,8]{0,1:T(8,128)S(1)}, f32[128,8]{0,1:T(8,128)S(1)}, f32[128,8,128]{2,0,1:T(8,128)S(1)}) %tuple.60, (f32[1,8]{1,0:T(1,128)S(1)}, s32[]{:T(128)}, s32[]{:T(128)}, ...), branch_computations={%region_4.4_spmd, %region_5.7_spmd.clone} | conditional | flops 551302400 | bytes 15061798 | solution.py:113
  182.7 1.0 fusion.10
  183.7 2.4 fusion.14
  187.5 5.2 %conditional.3 = ((f32[128,8]{0,1:T(8,128)S(1)}, f32[128,8]{0,1:T(8,128)S(1)}, f32[128,8,128]{2,0,1:T(8,128)S(1)})) conditional(s32[]{:T(128)} %convert_element_type.51, (f32[128,8]{0,1:T(8,128)S(1)}, f32[128,8]{0,1:T(8,128)S(1)}, f32[128,8,128]{2,0,1:T(8,128)S(1)}) %tuple.60, (f32[1,8]{1,0:T(1,128)S(1)}, s32[]{:T(128)}, s32[]{:T(128)}, ...), branch_computations={%region_4.4_spmd, %region_5.7_spmd.clone} | conditional | flops 551302400 | bytes 15061798 | solution.py:113
  190.3 2.4 fusion.14
  194.1 5.2 %conditional.3 = ((f32[128,8]{0,1:T(8,128)S(1)}, f32[128,8]{0,1:T(8,128)S(1)}, f32[128,8,128]{2,0,1:T(8,128)S(1)})) conditional(s32[]{:T(128)} %convert_element_type.51, (f32[128,8]{0,1:T(8,128)S(1)}, f32[128,8]{0,1:T(8,128)S(1)}, f32[128,8,128]{2,0,1:T(8,128)S(1)}) %tuple.60, (f32[1,8]{1,0:T(1,128)S(1)}, s32[]{:T(128)}, s32[]{:T(128)}, ...), branch_computations={%region_4.4_spmd, %region_5.7_spmd.clone} | conditional | flops 551302400 | bytes 15061798 | solution.py:113
  195.9 1.0 fusion.10
  196.9 2.4 fusion.14
  200.7 5.2 %conditional.3 = ((f32[128,8]{0,1:T(8,128)S(1)}, f32[128,8]{0,1:T(8,128)S(1)}, f32[128,8,128]{2,0,1:T(8,128)S(1)})) conditional(s32[]{:T(128)} %convert_element_type.51, (f32[128,8]{0,1:T(8,128)S(1)}, f32[128,8]{0,1:T(8,128)S(1)}, f32[128,8,128]{2,0,1:T(8,128)S(1)}) %tuple.60, (f32[1,8]{1,0:T(1,128)S(1)}, s32[]{:T(128)}, s32[]{:T(128)}, ...), branch_computations={%region_4.4_spmd, %region_5.7_spmd.clone} | conditional | flops 551302400 | bytes 15061798 | solution.py:113
  202.5 1.0 fusion.10
  203.5 2.4 fusion.14
  207.3 5.2 %conditional.3 = ((f32[128,8]{0,1:T(8,128)S(1)}, f32[128,8]{0,1:T(8,128)S(1)}, f32[128,8,128]{2,0,1:T(8,128)S(1)})) conditional(s32[]{:T(128)} %convert_element_type.51, (f32[128,8]{0,1:T(8,128)S(1)}, f32[128,8]{0,1:T(8,128)S(1)}, f32[128,8,128]{2,0,1:T(8,128)S(1)}) %tuple.60, (f32[1,8]{1,0:T(1,128)S(1)}, s32[]{:T(128)}, s32[]{:T(128)}, ...), branch_computations={%region_4.4_spmd, %region_5.7_spmd.clone} | conditional | flops 551302400 | bytes 15061798 | solution.py:113
  209.1 1.0 fusion.10
  210.1 2.4 fusion.14
  213.9 5.2 %conditional.3 = ((f32[128,8]{0,1:T(8,128)S(1)}, f32[128,8]{0,1:T(8,128)S(1)}, f32[128,8,128]{2,0,1:T(8,128)S(1)})) conditional(s32[]{:T(128)} %convert_element_type.51, (f32[128,8]{0,1:T(8,128)S(1)}, f32[128,8]{0,1:T(8,128)S(1)}, f32[128,8,128]{2,0,1:T(8,128)S(1)}) %tuple.60, (f32[1,8]{1,0:T(1,128)S(1)}, s32[]{:T(128)}, s32[]{:T(128)}, ...), branch_computations={%region_4.4_spmd, %region_5.7_spmd.clone} | conditional | flops 551302400 | bytes 15061798 | solution.py:113
  216.7 2.4 fusion.14
  220.5 5.2 %conditional.3 = ((f32[128,8]{0,1:T(8,128)S(1)}, f32[128,8]{0,1:T(8,128)S(1)}, f32[128,8,128]{2,0,1:T(8,128)S(1)})) conditional(s32[]{:T(128)} %convert_element_type.51, (f32[128,8]{0,1:T(8,128)S(1)}, f32[128,8]{0,1:T(8,128)S(1)}, f32[128,8,128]{2,0,1:T(8,128)S(1)}) %tuple.60, (f32[1,8]{1,0:T(1,128)S(1)}, s32[]{:T(128)}, s32[]{:T(128)}, ...), branch_computations={%region_4.4_spmd, %region_5.7_spmd.clone} | conditional | flops 551302400 | bytes 15061798 | solution.py:113
  222.2 1.0 fusion.10
  223.3 2.4 fusion.14
  227.1 5.2 %conditional.3 = ((f32[128,8]{0,1:T(8,128)S(1)}, f32[128,8]{0,1:T(8,128)S(1)}, f32[128,8,128]{2,0,1:T(8,128)S(1)})) conditional(s32[]{:T(128)} %convert_element_type.51, (f32[128,8]{0,1:T(8,128)S(1)}, f32[128,8]{0,1:T(8,128)S(1)}, f32[128,8,128]{2,0,1:T(8,128)S(1)}) %tuple.60, (f32[1,8]{1,0:T(1,128)S(1)}, s32[]{:T(128)}, s32[]{:T(128)}, ...), branch_computations={%region_4.4_spmd, %region_5.7_spmd.clone} | conditional | flops 551302400 | bytes 15061798 | solution.py:113
  229.9 2.4 fusion.14
  (182 shorter events, 29.3 us)
Async XLA Ops:
  6.5 1.0 copy-start
  6.5 27.4 %reduce-scatter.3.cloned.1.call-start = ((), (), s32[]{:S(2)}) async-start(), calls=%async_computation.2 | async-start | bytes 1572864 | tf_op jit(solution)/shard_map/reduce_scatter | solution.py:52
  10.4 105.5 %copy-start.1 = (bf16[128,1024]{1,0:T(8,128)(2,1)S(1)}, bf16[128,1024]{1,0:T(8,128)(2,1)}, u32[]{:S(2)}) copy-start(bf16[128,1024]{1,0:T(8,128)(2,1)} %param.11) | copy-start | bytes 786436
  10.4 105.9 %copy-start.3 = (s32[64]{0:T(128)S(1)}, s32[64]{0:T(128)}, u32[]{:S(2)}) copy-start(s32[64]{0:T(128)} %param.14) | copy-start | bytes 772
  10.4 107.1 %copy-start.2 = (s32[64]{0:T(128)S(1)}, s32[64]{0:T(128)}, u32[]{:S(2)}) copy-start(s32[64]{0:T(128)} %param.15) | copy-start | bytes 772
  12.7 56.4 %reduce-scatter.5.cloned.1.call-start = ((), (), s32[]{:S(2)}) async-start(), calls=%async_computation.3 | async-start | bytes 655360 | tf_op jit(solution)/shard_map/reduce_scatter | solution.py:53
  34.0 81.8 %all-gather.3.cloned.1.call-start = ((), (), s32[]{:S(2)}) async-start(), calls=%async_computation.4 | async-start | bytes 1179648 | tf_op jit(solution)/shard_map/all_gather | solution.py:68
  75.2 93.8 %all-gather.5.cloned.1.call-start = ((), (), s32[]{:S(2)}) async-start(), calls=%async_computation.5 | async-start | bytes 5242880 | tf_op jit(solution)/shard_map/all_gather | solution.py:69
Sparse Core Ops, SparseCore 0:
  12.8 21.1 reduce-scatter.2
  36.8 32.2 reduce-scatter.4
  75.3 40.5 all-gather.2
  117.8 51.1 all-gather.4

commit v2 on v1

v2 whole, which is shorter than its diff:
```python
import math

import jax
import jax.numpy as jnp
import numpy as np
from jax import lax
from jax.experimental import pallas as pl
from jax.experimental.pallas import tpu as pltpu
from jax.sharding import Mesh
from jax.sharding import PartitionSpec as P

HD = 128
BLOCK = 128
FSDP_AXES = ("zh", "c")
SEQ_AXES = ("zl", "x", "y")


def ancestry_table(parents, slot_block):
    block_count = parents.shape[0]
    block_ids = jnp.arange(block_count, dtype=jnp.int32)
    linked = (parents[:, None] == block_ids[None, :]).astype(jnp.float32)
    ancestry = jnp.maximum(jnp.eye(block_count, dtype=jnp.float32), linked)
    for sweep in range(block_count.bit_length()):
        ancestry = jnp.minimum(jnp.dot(ancestry, ancestry, precision=lax.Precision.HIGHEST), 1.0)
    placement = (slot_block[:, None] == block_ids[None, :]).astype(jnp.float32)
    first_pass = jnp.dot(placement, ancestry, precision=lax.Precision.HIGHEST)
    return jnp.dot(first_pass, placement.T, precision=lax.Precision.HIGHEST)


def seq_index():
    return (lax.axis_index("zl") * lax.axis_size("x") + lax.axis_index("x")) * lax.axis_size("y") + lax.axis_index("y")


def fsdp_index():
    return lax.axis_index("zh") * lax.axis_size("c") + lax.axis_index("c")


def shards(hidden, queries, kv_weight, kv_bias, parents, slot_block):
    tok_rows = hidden.shape[0]
    per_device = tok_rows // BLOCK
    head_count = queries.shape[1] // HD
    score_scale = 1.0 / math.sqrt(HD)
    f_index = fsdp_index()
    n_zh = lax.axis_size("zh")
    n_c = lax.axis_size("c")
    partial_sums = jnp.dot(hidden, kv_weight, preferred_element_type=jnp.float32)
    cols = partial_sums.shape[1]
    per_head = cols // (n_zh * n_c)
    regrouped = partial_sums.reshape(tok_rows, n_zh, n_c, per_head).transpose(0, 2, 1, 3).reshape(tok_rows, cols)
    half = lax.psum_scatter(regrouped, "c", scatter_dimension=1, tiled=True)
    head_cols = lax.psum_scatter(half, "zh", scatter_dimension=1, tiled=True)
    head_bias = lax.dynamic_slice_in_dim(kv_bias, f_index * 2 * HD, 2 * HD, 0)
    both_parts = (head_cols + head_bias).astype(jnp.bfloat16)
    visible = ancestry_table(parents, slot_block)
    first_slot = seq_index() * per_device
    own_visible = lax.dynamic_slice_in_dim(visible, first_slot, per_device, 0)
    gathered = lax.all_gather(both_parts, "zl", axis=0, tiled=True)
    gathered = lax.all_gather(gathered, "y", axis=0, tiled=True)
    gathered = lax.all_gather(gathered, "x", axis=0, tiled=True)
    n_zl, n_x, n_y = lax.axis_size("zl"), lax.axis_size("x"), lax.axis_size("y")
    own_slot = first_slot
    slots = jnp.arange(visible.shape[1], dtype=jnp.int32)
    slot_zl = slots // (n_x * n_y)
    slot_x = (slots // n_y) % n_x
    slot_y = slots % n_y
    physical = (slot_x * n_y + slot_y) * n_zl + slot_zl
    seen = own_visible[0] > 0.5
    count = jnp.sum(seen.astype(jnp.int32))
    position = jnp.cumsum(seen.astype(jnp.int32)) - 1
    wanted = jnp.minimum(slots, count - 1)
    hit = seen[None, :] & (position[None, :] == wanted[:, None])
    order = jnp.sum(jnp.where(hit, slots[None, :], 0), axis=1).astype(jnp.int32)
    order_physical = physical[order]
    diagonal = (order == own_slot).astype(jnp.int32)
    return attention(order_physical, diagonal, count.reshape(1), queries, gathered, head_count, score_scale)


def attention(order_physical, diagonal, count, queries, kv, head_count, score_scale):
    tok_rows = queries.shape[0]
    rows = tok_rows * head_count
    steps = order_physical.shape[0]

    def kernel(order_ref, diag_ref, count_ref, q_ref, kv_ref, o_ref, q_scr, m_scr, l_scr, acc_scr):
        i = pl.program_id(0)

        @pl.when(i == 0)
        def _():
            for h in range(head_count):
                q_scr[h * tok_rows:(h + 1) * tok_rows, :] = q_ref[:, h * HD:(h + 1) * HD]
            m_scr[...] = jnp.full(m_scr.shape, -1e30, jnp.float32)
            l_scr[...] = jnp.zeros(l_scr.shape, jnp.float32)
            acc_scr[...] = jnp.zeros(acc_scr.shape, jnp.float32)

        @pl.when(i < count_ref[0])
        def _():
            kv_blk = kv_ref[...]
            k_blk = kv_blk[:, :HD]
            v_blk = kv_blk[:, HD:]
            scores = lax.dot_general(
                q_scr[...], k_blk, (((1,), (1,)), ((), ())), preferred_element_type=jnp.float32
            ) * score_scale
            tok = lax.broadcasted_iota(jnp.int32, (rows, BLOCK), 0) % tok_rows
            key = lax.broadcasted_iota(jnp.int32, (rows, BLOCK), 1)
            allowed = (key <= tok) | (diag_ref[i] == 0)
            scores = jnp.where(allowed, scores, -1e30)
            m_old = m_scr[...]
            m_new = jnp.maximum(m_old, jnp.max(scores, axis=1, keepdims=True))
            expo = jnp.exp(scores - m_new)
            factor = jnp.exp(m_old - m_new)
            l_scr[...] = l_scr[...] * factor + jnp.sum(expo, axis=1, keepdims=True)
            acc_scr[...] = acc_scr[...] * factor + jnp.dot(
                expo.astype(jnp.bfloat16), v_blk, preferred_element_type=jnp.float32
            )
            m_scr[...] = m_new

        @pl.when(i == steps - 1)
        def _():
            result = acc_scr[...] / l_scr[...]
            for h in range(head_count):
                o_ref[:, h * HD:(h + 1) * HD] = result[h * tok_rows:(h + 1) * tok_rows].astype(o_ref.dtype)

    grid_spec = pltpu.PrefetchScalarGridSpec(
        num_scalar_prefetch=3,
        grid=(steps,),
        in_specs=[
            pl.BlockSpec((tok_rows, head_count * HD), lambda i, o, d, c: (0, 0)),
            pl.BlockSpec((BLOCK, 2 * HD), lambda i, o, d, c: (o[i], 0)),
        ],
        out_specs=pl.BlockSpec((tok_rows, head_count * HD), lambda i, o, d, c: (0, 0)),
        scratch_shapes=[
            pltpu.VMEM((rows, HD), jnp.bfloat16),
            pltpu.VMEM((rows, 1), jnp.float32),
            pltpu.VMEM((rows, 1), jnp.float32),
            pltpu.VMEM((rows, HD), jnp.float32),
        ],
    )
    return pl.pallas_call(
        kernel,
        grid_spec=grid_spec,
        out_shape=jax.ShapeDtypeStruct((tok_rows, head_count * HD), jnp.bfloat16),
        compiler_params=pltpu.CompilerParams(dimension_semantics=("arbitrary",)),
    )(order_physical, diagonal, count, queries, kv)


def solution(mesh):
    n_fsdp, n_seq = mesh.devices.shape
    n_c = 2
    n_zh = n_fsdp // n_c
    n_zl = 2
    n_y = 8
    n_x = n_seq // (n_zl * n_y)
    fine = Mesh(mesh.devices.reshape(n_zh, n_c, n_zl, n_x, n_y), FSDP_AXES + SEQ_AXES)
    tok = P(SEQ_AXES, FSDP_AXES)
    return jax.shard_map(
        shards,
        mesh=fine,
        in_specs=(tok, tok, P(FSDP_AXES, None), P(), P(), P()),
        out_specs=tok,
        check_vma=False,
    )
```

time: 243 us -> 265 us (1.091)
  the two profiles are of different devices: /device:TPU:6 before, /device:TPU:1 now
where the time goes in v2:
time: 265 us; the launch traced here: 264 us
  waiting for transfers between devices  146 us (55%)
  Pallas kernels  87.6 us (33%)
  between operations  14 us (5%)
  local copies, waits for them, and re-layouts  5.86 us (2%)
  matrix products  4.55 us (2%)
  blocking collectives  3.89 us (1%)
    pallas_call x1, Pallas kernels, attention(): pl.pallas_call(kernel, grid_spec=grid_spec, out_shape=jax.ShapeDtypeStruc...  87.6 us
    all_gather x1, waiting for transfers between devices, shards(): gathered = lax.all_gather(gathered, 'x', axis=0, tiled=True)  53.6 us
    all_gather x1, waiting for transfers between devices, shards(): gathered = lax.all_gather(gathered, 'y', axis=0, tiled=True)  37.2 us
    reduce_scatter x1, waiting for transfers between devices, shards(): head_cols = lax.psum_scatter(half, 'zh', scatter_dimension=1, tiled=True)  31.5 us
    reduce_scatter x1, waiting for transfers between devices, shards(): half = lax.psum_scatter(regrouped, 'c', scatter_dimension=1, tiled=True)  23.5 us
  transfers between devices with their start and end apart: 4, of which 4 were waited for; matrix products, arithmetic and copies ran while one was open for 2% of the time, Pallas kernels for 0%

profile of v2, /device:TPU:1, one launch (start us, length us, event | category | flops | bytes accessed | tf_op | source)
XLA Modules:
  0.0 264.5 jit_solution(16085712571744323835)
XLA Ops:
  6.5 0.9 copy-done
  7.5 2.9 %fusion.16 = f32[128,2048]{1,0:T(8,128)S(1)} fusion(bf16[128,1024]{1,0:T(8,128)(2,1)S(1)} %copy-done, bf16[1024,2048]{1,0:T(8,128)(2,1)} %param.8), kind=kOutput, calls=%fused_computation.49 | convolution fusion | flops 536870912 | bytes 5505024 | tf_op jit(solution)/shard_map/dot_general | solution.py:46
  10.4 0.9 reshape.65
  11.3 0.3 copy.14
  11.6 1.5 reshape.66
  13.1 0.0 reduce-scatter.5.cloned.1.call-start
  13.2 23.5 %reduce-scatter.3.cloned.1.call-done = f32[128,1024]{1,0:T(8,128)} async-done(((f32[128,2048]{1,0:T(8,128)}), f32[128,1024]{1,0:T(8,128)}) %reduce-scatter.3.cloned.1.call-update) | async-done | bytes 524304 | tf_op jit(solution)/shard_map/reduce_scatter | solution.py:50
  36.8 0.0 all-gather.3.cloned.1.call-start
  36.8 0.8 dynamic_slice.7
  37.6 31.5 %reduce-scatter.5.cloned.1.call-done = f32[128,256]{1,0:T(8,128)} async-done(((f32[128,1024]{1,0:T(8,128)}), f32[128,256]{1,0:T(8,128)}) %reduce-scatter.5.cloned.1.call-update) | async-done | bytes 131088 | tf_op jit(solution)/shard_map/reduce_scatter | solution.py:51
  69.1 0.9 add_convert_fusion
  70.0 3.9 %all_gather.9 = bf16[256,256]{1,0:T(8,128)(2,1)} all-gather(bf16[128,256]{1,0:T(8,128)(2,1)S(1)} %add_convert_fusion), channel_id=1, replica_groups=mesh['zh'=4,'c'=2,'zl'=2,'x'=4,'y'=8] {'zl'}, dimensions={0}, use_global_device_ids=true | all-gather | bytes 196608 | tf_op jit(solution)/shard_map/all_gather | solution.py:57
  73.9 0.0 all-gather.5.cloned.1.call-start
  73.9 37.2 %all-gather.3.cloned.1.call-done = bf16[2048,256]{1,0:T(8,128)(2,1)} async-done(((bf16[256,256]{1,0:T(8,128)(2,1)}), bf16[2048,256]{1,0:T(8,128)(2,1)}) %all-gather.3.cloned.1.call-update) | async-done | bytes 1048592 | tf_op jit(solution)/shard_map/all_gather | solution.py:58
  111.2 0.2 convolution_minimum_fusion.6
  111.4 0.2 convolution_minimum_fusion.5
  111.6 0.2 convolution_minimum_fusion.4
  111.8 0.2 convolution_minimum_fusion.3
  111.9 0.2 convolution_minimum_fusion.2
  112.1 0.2 convolution_minimum_fusion.1
  112.3 0.2 convolution_minimum_fusion
  112.5 0.2 fusion.4
  112.7 0.2 fusion.3
  112.9 0.1 copy.11
  113.0 0.1 reduce-window.8
  113.1 0.7 fusion.14
  114.5 0.1 add_reduce_fusion
  114.6 0.2 select_reduce_fusion
  114.8 1.4 gather_fusion
  116.1 0.6 compare_convert_fusion.diag_ref
  116.7 53.6 %all-gather.5.cloned.1.call-done.kv_ref = bf16[8192,256]{1,0:T(8,128)(2,1)} async-done(((bf16[2048,256]{1,0:T(8,128)(2,1)}), bf16[8192,256]{1,0:T(8,128)(2,1)}) %all-gather.5.cloned.1.call-update) | async-done | bytes 4194320 | tf_op jit(solution)/shard_map/all_gather | solution.py:59
  170.3 87.6 %shard_map.64 = bf16[128,1024]{1,0:T(8,128)(2,1)} custom-call(s32[64]{0:T(128)} %gather_fusion, s32[64]{0:T(128)} %compare_convert_fusion.diag_ref, s32[1]{0:T(128)} %bitcast.4.count_ref, bf16[128,1024]{1,0:T(8,128)(2,1)} %q_ref.1, bf16[8192,256]{1,0:T(8,128)(2,1)} %all-gather.5.cloned.1.call-done.kv_ref), custom_call_target="tpu_custom_call" | custom-call | tf_op jit(solution)/shard_map/pallas_call | solution.py:137
  (15 shorter events, 0.1 us)
Async XLA Ops:
  6.5 1.0 copy-start
  6.5 30.2 %reduce-scatter.3.cloned.1.call-start = ((), (), s32[]{:S(2)}) async-start(), calls=%async_computation.2 | async-start | bytes 1572864 | tf_op jit(solution)/shard_map/reduce_scatter | solution.py:50
  11.3 99.9 %copy-start.2 = (s32[64]{0:T(128)S(1)}, s32[64]{0:T(128)}, u32[]{:S(2)}) copy-start(s32[64]{0:T(128)} %param.10) | copy-start | bytes 772
  11.3 101.1 %copy-start.1 = (s32[64]{0:T(128)S(1)}, s32[64]{0:T(128)}, u32[]{:S(2)}) copy-start(s32[64]{0:T(128)} %param.11) | copy-start | bytes 772
  13.1 55.9 %reduce-scatter.5.cloned.1.call-start = ((), (), s32[]{:S(2)}) async-start(), calls=%async_computation.3 | async-start | bytes 655360 | tf_op jit(solution)/shard_map/reduce_scatter | solution.py:51
  36.8 74.4 %all-gather.3.cloned.1.call-start = ((), (), s32[]{:S(2)}) async-start(), calls=%async_computation.4 | async-start | bytes 1179648 | tf_op jit(solution)/shard_map/all_gather | solution.py:58
  73.9 96.4 %all-gather.5.cloned.1.call-start = ((), (), s32[]{:S(2)}) async-start(), calls=%async_computation.5 | async-start | bytes 5242880 | tf_op jit(solution)/shard_map/all_gather | solution.py:59
Sparse Core Ops, SparseCore 0:
  13.3 23.4 reduce-scatter.2
  39.6 29.4 reduce-scatter.4
  74.0 37.0 all-gather.2
  113.1 57.1 all-gather.4

commit v3 on v2

v3 whole, which is shorter than its diff:
```python
import math

import jax
import jax.numpy as jnp
import numpy as np
from jax import lax
from jax.experimental import pallas as pl
from jax.experimental.pallas import tpu as pltpu
from jax.sharding import Mesh
from jax.sharding import PartitionSpec as P

HD = 128
BLOCK = 128
FSDP_AXES = ("zh", "c")
SEQ_AXES = ("zl", "x", "y")


def ancestry_table(parents, slot_block):
    block_count = parents.shape[0]
    block_ids = jnp.arange(block_count, dtype=jnp.int32)
    linked = (parents[:, None] == block_ids[None, :]).astype(jnp.float32)
    ancestry = jnp.maximum(jnp.eye(block_count, dtype=jnp.float32), linked)
    for sweep in range(block_count.bit_length()):
        ancestry = jnp.minimum(jnp.dot(ancestry, ancestry, precision=lax.Precision.HIGHEST), 1.0)
    placement = (slot_block[:, None] == block_ids[None, :]).astype(jnp.float32)
    first_pass = jnp.dot(placement, ancestry, precision=lax.Precision.HIGHEST)
    return jnp.dot(first_pass, placement.T, precision=lax.Precision.HIGHEST)


def seq_index():
    return (lax.axis_index("zl") * lax.axis_size("x") + lax.axis_index("x")) * lax.axis_size("y") + lax.axis_index("y")


def fsdp_index():
    return lax.axis_index("zh") * lax.axis_size("c") + lax.axis_index("c")


def shards(hidden, queries, kv_weight, kv_bias, parents, slot_block):
    tok_rows = hidden.shape[0]
    per_device = tok_rows // BLOCK
    head_count = queries.shape[1] // HD
    score_scale = 1.0 / math.sqrt(HD)
    f_index = fsdp_index()
    n_zh = lax.axis_size("zh")
    n_c = lax.axis_size("c")
    partial_sums = jnp.dot(hidden, kv_weight, preferred_element_type=jnp.float32)
    cols = partial_sums.shape[1]
    per_head = cols // (n_zh * n_c)
    regrouped = partial_sums.reshape(tok_rows, n_zh, n_c, per_head).transpose(0, 2, 1, 3).reshape(tok_rows, cols)
    half = lax.psum_scatter(regrouped, "c", scatter_dimension=1, tiled=True)
    head_cols = lax.psum_scatter(half, "zh", scatter_dimension=1, tiled=True)
    head_bias = lax.dynamic_slice_in_dim(kv_bias, f_index * 2 * HD, 2 * HD, 0)
    both_parts = (head_cols + head_bias).astype(jnp.bfloat16)
    kv_block = jnp.concatenate([both_parts[:, :HD], both_parts[:, HD:].T], axis=0)
    visible = ancestry_table(parents, slot_block)
    own_slot = seq_index() * per_device
    own_visible = lax.dynamic_slice_in_dim(visible, own_slot, per_device, 0)
    gathered = lax.all_gather(kv_block, "zl", axis=0, tiled=True)
    gathered = lax.all_gather(gathered, "y", axis=0, tiled=True)
    gathered = lax.all_gather(gathered, "x", axis=0, tiled=True)
    n_zl, n_x, n_y = lax.axis_size("zl"), lax.axis_size("x"), lax.axis_size("y")
    slots = jnp.arange(visible.shape[1], dtype=jnp.int32)
    slot_zl = slots // (n_x * n_y)
    slot_x = (slots // n_y) % n_x
    slot_y = slots % n_y
    physical = (slot_x * n_y + slot_y) * n_zl + slot_zl
    others = (own_visible[0] > 0.5) & (slots != own_slot)
    count = jnp.sum(others.astype(jnp.int32)) + 1
    position = jnp.cumsum(others.astype(jnp.int32))
    wanted = jnp.minimum(slots, count - 1)
    hit = others[None, :] & (position[None, :] == wanted[:, None])
    order = jnp.where(wanted == 0, own_slot, jnp.sum(jnp.where(hit, slots[None, :], 0), axis=1))
    order_physical = physical[order].astype(jnp.int32)
    return attention(order_physical, count.reshape(1), queries, gathered, head_count, score_scale)


def attention(order_physical, count, queries, kv, head_count, score_scale):
    tok_rows = queries.shape[0]
    rows = tok_rows * head_count
    steps = order_physical.shape[0] // 2

    def kernel(order_ref, count_ref, q_ref, kva_ref, kvb_ref, o_ref, q_scr, m_scr, l_scr, acc_scr):
        i = pl.program_id(0)

        @pl.when(i == 0)
        def _():
            for h in range(head_count):
                q_h = q_ref[:, h * HD:(h + 1) * HD].astype(jnp.float32)
                q_scr[:, h * tok_rows:(h + 1) * tok_rows] = q_h.T.astype(jnp.bfloat16)
            m_scr[...] = jnp.full(m_scr.shape, -1e30, jnp.float32)
            l_scr[...] = jnp.zeros(l_scr.shape, jnp.float32)
            acc_scr[...] = jnp.zeros(acc_scr.shape, jnp.float32)

        def scores_of(kv_ref, causal):
            s_t = jnp.dot(kv_ref[:BLOCK, :], q_scr[...], preferred_element_type=jnp.float32) * score_scale
            if causal:
                key = lax.broadcasted_iota(jnp.int32, (BLOCK, rows), 0)
                tok = lax.broadcasted_iota(jnp.int32, (BLOCK, rows), 1) % tok_rows
                s_t = jnp.where(key <= tok, s_t, -1e30)
            return s_t

        def step(first_causal, with_second):
            parts = [(scores_of(kva_ref, first_causal), kva_ref)]
            if with_second:
                parts.append((scores_of(kvb_ref, False), kvb_ref))
            m_old = m_scr[...]
            m_new = m_old
            for s_t, _ in parts:
                m_new = jnp.maximum(m_new, jnp.max(s_t, axis=0, keepdims=True))
            factor = jnp.exp(m_old - m_new)
            l_new = l_scr[...] * factor
            acc_new = acc_scr[...] * factor
            for s_t, ref in parts:
                expo = jnp.exp(s_t - m_new)
                l_new = l_new + jnp.sum(expo, axis=0, keepdims=True)
                acc_new = acc_new + jnp.dot(ref[BLOCK:, :], expo.astype(jnp.bfloat16), preferred_element_type=jnp.float32)
            l_scr[...] = l_new
            acc_scr[...] = acc_new
            m_scr[...] = m_new

        n = count_ref[0]
        second = 2 * i + 1 < n

        @pl.when((i == 0) & second)
        def _():
            step(True, True)

        @pl.when((i == 0) & jnp.logical_not(second))
        def _():
            step(True, False)

        @pl.when((i > 0) & second)
        def _():
            step(False, True)

        @pl.when((i > 0) & (2 * i < n) & jnp.logical_not(second))
        def _():
            step(False, False)

        @pl.when(i == steps - 1)
        def _():
            for h in range(head_count):
                cols = slice(h * tok_rows, (h + 1) * tok_rows)
                result = acc_scr[:, cols] / l_scr[:, cols]
                o_ref[:, h * HD:(h + 1) * HD] = result.T.astype(o_ref.dtype)

    grid_spec = pltpu.PrefetchScalarGridSpec(
        num_scalar_prefetch=2,
        grid=(steps,),
        in_specs=[
            pl.BlockSpec((tok_rows, head_count * HD), lambda i, o, c: (0, 0)),
            pl.BlockSpec((2 * BLOCK, HD), lambda i, o, c: (o[2 * i], 0)),
            pl.BlockSpec((2 * BLOCK, HD), lambda i, o, c: (o[2 * i + 1], 0)),
        ],
        out_specs=pl.BlockSpec((tok_rows, head_count * HD), lambda i, o, c: (0, 0)),
        scratch_shapes=[
            pltpu.VMEM((HD, rows), jnp.bfloat16),
            pltpu.VMEM((1, rows), jnp.float32),
            pltpu.VMEM((1, rows), jnp.float32),
            pltpu.VMEM((HD, rows), jnp.float32),
        ],
    )
    return pl.pallas_call(
        kernel,
        grid_spec=grid_spec,
        out_shape=jax.ShapeDtypeStruct((tok_rows, head_count * HD), jnp.bfloat16),
        compiler_params=pltpu.CompilerParams(dimension_semantics=("arbitrary",)),
    )(order_physical, count, queries, kv, kv)


def solution(mesh):
    n_fsdp, n_seq = mesh.devices.shape
    n_c = 2
    n_zh = n_fsdp // n_c
    n_zl = 2
    n_y = 8
    n_x = n_seq // (n_zl * n_y)
    fine = Mesh(mesh.devices.reshape(n_zh, n_c, n_zl, n_x, n_y), FSDP_AXES + SEQ_AXES)
    tok = P(SEQ_AXES, FSDP_AXES)
    return jax.shard_map(
        shards,
        mesh=fine,
        in_specs=(tok, tok, P(FSDP_AXES, None), P(), P(), P()),
        out_specs=tok,
        check_vma=False,
    )
```

time: 265 us -> 205 us (0.77)
  Pallas kernels: 87.6 us -> 27.2 us
    pallas_call x1, Pallas kernels: 87.6 us -> 27.2 us  [attention(): pl.pallas_call(kernel, grid_spec=grid_spec, out_shape=jax.ShapeDtypeStruc...]
  transfers between devices with their start and end apart: 4 -> 4, of which waited for: 4 -> 4; matrix products, arithmetic and copies ran while one was open for 2% -> 3% of each run, Pallas kernels for 0% -> 0%
where the time goes in v3:
time: 205 us; the launch traced here: 204 us
  waiting for transfers between devices  145 us (71%)
  Pallas kernels  27.2 us (13%)
  between operations  14 us (7%)
  local copies, waits for them, and re-layouts  5.44 us (3%)
  matrix products  4.55 us (2%)
  blocking collectives  3.89 us (2%)
  other arithmetic  3.37 us (2%)
    all_gather x1, waiting for transfers between devices, shards(): gathered = lax.all_gather(gathered, 'x', axis=0, tiled=True)  52.9 us
    all_gather x1, waiting for transfers between devices, shards(): gathered = lax.all_gather(gathered, 'y', axis=0, tiled=True)  37.3 us
    reduce_scatter x1, waiting for transfers between devices, shards(): head_cols = lax.psum_scatter(half, 'zh', scatter_dimension=1, tiled=True)  31.5 us
    pallas_call x1, Pallas kernels, attention(): pl.pallas_call(kernel, grid_spec=grid_spec, out_shape=jax.ShapeDtypeStruc...  27.2 us
    reduce_scatter x1, waiting for transfers between devices, shards(): half = lax.psum_scatter(regrouped, 'c', scatter_dimension=1, tiled=True)  23.5 us
  transfers between devices with their start and end apart: 4, of which 4 were waited for; matrix products, arithmetic and copies ran while one was open for 3% of the time, Pallas kernels for 0%

profile of v3, /device:TPU:1, one launch (start us, length us, event | category | flops | bytes accessed | tf_op | source)
XLA Modules:
  0.0 203.9 jit_solution(1104307384386520989)
XLA Ops:
  6.5 0.9 copy-done
  7.5 2.9 %fusion.17 = f32[128,2048]{1,0:T(8,128)S(1)} fusion(bf16[128,1024]{1,0:T(8,128)(2,1)S(1)} %copy-done, bf16[1024,2048]{1,0:T(8,128)(2,1)} %param.8), kind=kOutput, calls=%fused_computation.51 | convolution fusion | flops 536870912 | bytes 5505024 | tf_op jit(solution)/shard_map/dot_general | solution.py:46
  10.4 0.9 reshape.85
  11.3 1.3 copy.14
  12.6 0.0 reduce-scatter.5.cloned.1.call-start
  12.7 23.5 %reduce-scatter.3.cloned.1.call-done = f32[128,1024]{0,1:T(8,128)} async-done(((f32[128,2048]{0,1:T(8,128)}), f32[128,1024]{0,1:T(8,128)}) %reduce-scatter.3.cloned.1.call-update) | async-done | bytes 524304 | tf_op jit(solution)/shard_map/reduce_scatter | solution.py:50
  36.3 0.8 dynamic_slice.7
  37.1 31.5 %reduce-scatter.5.cloned.1.call-done = f32[128,256]{0,1:T(8,128)} async-done(((f32[128,1024]{0,1:T(8,128)}), f32[128,256]{0,1:T(8,128)}) %reduce-scatter.5.cloned.1.call-update) | async-done | bytes 131088 | tf_op jit(solution)/shard_map/reduce_scatter | solution.py:51
  68.6 1.0 add_convert_fusion
  69.6 0.1 copy.15
  69.8 3.9 %all_gather.9 = bf16[512,128]{1,0:T(8,128)(2,1)} all-gather(bf16[256,128]{1,0:T(8,128)(2,1)S(1)} %pad_maximum_fusion), channel_id=1, replica_groups=mesh['zh'=4,'c'=2,'zl'=2,'x'=4,'y'=8] {'zl'}, dimensions={0}, use_global_device_ids=true | all-gather | bytes 196608 | tf_op jit(solution)/shard_map/all_gather | solution.py:58
  73.7 0.0 all-gather.5.cloned.1.call-start
  73.7 37.3 %all-gather.3.cloned.1.call-done = bf16[4096,128]{1,0:T(8,128)(2,1)} async-done(((bf16[512,128]{1,0:T(8,128)(2,1)}), bf16[4096,128]{1,0:T(8,128)(2,1)}) %all-gather.3.cloned.1.call-update) | async-done | bytes 1048592 | tf_op jit(solution)/shard_map/all_gather | solution.py:59
  111.0 0.2 convolution_minimum_fusion.6
  111.3 0.2 convolution_minimum_fusion.5
  111.4 0.2 convolution_minimum_fusion.4
  111.6 0.2 convolution_minimum_fusion.3
  111.8 0.2 convolution_minimum_fusion.2
  111.9 0.2 convolution_minimum_fusion.1
  112.1 0.2 convolution_minimum_fusion
  112.3 0.2 fusion.4
  112.5 0.2 fusion.3
  112.8 0.1 copy.13
  112.9 0.1 reduce-window.8
  113.0 0.1 reduce
  113.1 0.6 fusion.14
  114.4 0.7 iota_minimum_fusion
  115.0 0.2 select_reduce_fusion
  115.2 0.7 fusion.15
  115.9 1.3 gather_fusion
  117.2 52.9 %all-gather.5.cloned.1.call-done.kva_ref.kvb_ref = bf16[16384,128]{1,0:T(8,128)(2,1)} async-done(((bf16[4096,128]{1,0:T(8,128)(2,1)}), bf16[16384,128]{1,0:T(8,128)(2,1)}) %all-gather.5.cloned.1.call-update) | async-done | bytes 4194320 | tf_op jit(solution)/shard_map/all_gather | solution.py:60
  170.1 27.2 %shard_map.64 = bf16[128,1024]{1,0:T(8,128)(2,1)} custom-call(s32[64]{0:T(128)} %gather_fusion, s32[1]{0:T(128)} %bitcast.5.count_ref, bf16[128,1024]{1,0:T(8,128)(2,1)} %q_ref.1, bf16[16384,128]{1,0:T(8,128)(2,1)} %all-gather.5.cloned.1.call-done.kva_ref.kvb_ref, bf16[16384,128]{1,0:T(8,128)(2,1)} %all-gather.5.cloned.1.call-done.kva_ref.kvb_ref), custom_call_target="tpu_custom_call" | custom-call | tf_op jit(solution)/shard_map/pallas_call | solution.py:163
  (16 shorter events, 0.2 us)
Async XLA Ops:
  6.5 1.0 copy-start
  6.5 29.7 %reduce-scatter.3.cloned.1.call-start = ((), (), s32[]{:S(2)}) async-start(), calls=%async_computation.2 | async-start | bytes 1572864 | tf_op jit(solution)/shard_map/reduce_scatter | solution.py:50
  10.4 100.6 %copy-start.2 = (s32[64]{0:T(128)S(1)}, s32[64]{0:T(128)}, u32[]{:S(2)}) copy-start(s32[64]{0:T(128)} %param.10) | copy-start | bytes 772
  10.4 101.9 %copy-start.1 = (s32[64]{0:T(128)S(1)}, s32[64]{0:T(128)}, u32[]{:S(2)}) copy-start(s32[64]{0:T(128)} %param.11) | copy-start | bytes 772
  12.6 56.0 %reduce-scatter.5.cloned.1.call-start = ((), (), s32[]{:S(2)}) async-start(), calls=%async_computation.3 | async-start | bytes 655360 | tf_op jit(solution)/shard_map/reduce_scatter | solution.py:51
  36.3 74.7 %all-gather.3.cloned.1.call-start = ((), (), s32[]{:S(2)}) async-start(), calls=%async_computation.4 | async-start | bytes 1179648 | tf_op jit(solution)/shard_map/all_gather | solution.py:59
  73.7 96.5 %all-gather.5.cloned.1.call-start = ((), (), s32[]{:S(2)}) async-start(), calls=%async_computation.5 | async-start | bytes 5242880 | tf_op jit(solution)/shard_map/all_gather | solution.py:60
Sparse Core Ops, SparseCore 0:
  12.8 23.4 reduce-scatter.2
  39.0 29.5 reduce-scatter.4
  73.8 37.1 all-gather.2
  112.9 57.1 all-gather.4

commit v4 on v3

--- a/solution.py
+++ b/solution.py
@@ -56,8 +56,7 @@
     own_slot = seq_index() * per_device
     own_visible = lax.dynamic_slice_in_dim(visible, own_slot, per_device, 0)
     gathered = lax.all_gather(kv_block, "zl", axis=0, tiled=True)
-    gathered = lax.all_gather(gathered, "y", axis=0, tiled=True)
-    gathered = lax.all_gather(gathered, "x", axis=0, tiled=True)
+    gathered = lax.all_gather(gathered, ("x", "y"), axis=0, tiled=True)
     n_zl, n_x, n_y = lax.axis_size("zl"), lax.axis_size("x"), lax.axis_size("y")
     slots = jnp.arange(visible.shape[1], dtype=jnp.int32)
     slot_zl = slots // (n_x * n_y)

time: 205 us -> 188 us (0.917)
  the two profiles are of different devices: /device:TPU:1 before, /device:TPU:64 now
where the time goes in v4:
time: 188 us; the launch traced here: 187 us
  waiting for transfers between devices  135 us (72%)
  Pallas kernels  20 us (11%)
  between operations  14 us (7%)
  local copies, waits for them, and re-layouts  5.45 us (3%)
  blocking collectives  5.04 us (3%)
  matrix products  4.55 us (2%)
  other arithmetic  3.37 us (2%)
    all_gather x1, waiting for transfers between devices, shards(): gathered = lax.all_gather(gathered, ('x', 'y'), axis=0, tiled=True)  80.9 us
    reduce_scatter x1, waiting for transfers between devices, shards(): head_cols = lax.psum_scatter(half, 'zh', scatter_dimension=1, tiled=True)  33.1 us
    reduce_scatter x1, waiting for transfers between devices, shards(): half = lax.psum_scatter(regrouped, 'c', scatter_dimension=1, tiled=True)  20.6 us
    pallas_call x1, Pallas kernels, attention(): pl.pallas_call(kernel, grid_spec=grid_spec, out_shape=jax.ShapeDtypeStruc...  20 us
    all_gather x1, blocking collectives, shards(): gathered = lax.all_gather(kv_block, 'zl', axis=0, tiled=True)  5.04 us
  transfers between devices with their start and end apart: 3, of which 3 were waited for; matrix products, arithmetic and copies ran while one was open for 3% of the time, Pallas kernels for 0%

profile of v4, /device:TPU:64, one launch (start us, length us, event | category | flops | bytes accessed | tf_op | source)
XLA Modules:
  0.0 187.1 jit_solution(9837776461527008993)
XLA Ops:
  6.5 0.9 copy-done
  7.5 2.9 %fusion.17 = f32[128,2048]{1,0:T(8,128)S(1)} fusion(bf16[128,1024]{1,0:T(8,128)(2,1)S(1)} %copy-done, bf16[1024,2048]{1,0:T(8,128)(2,1)} %param.8), kind=kOutput, calls=%fused_computation.51 | convolution fusion | flops 536870912 | bytes 5505024 | tf_op jit(solution)/shard_map/dot_general | solution.py:46
  10.4 0.9 reshape.85
  11.3 1.3 copy.14
  12.6 0.0 reduce-scatter.5.cloned.1.call-start
  12.7 20.6 %reduce-scatter.3.cloned.1.call-done = f32[128,1024]{0,1:T(8,128)} async-done(((f32[128,2048]{0,1:T(8,128)}), f32[128,1024]{0,1:T(8,128)}) %reduce-scatter.3.cloned.1.call-update) | async-done | bytes 524304 | tf_op jit(solution)/shard_map/reduce_scatter | solution.py:50
  33.3 0.0 all-gather.2.cloned.1.call-start
  33.4 0.8 dynamic_slice.7
  34.1 33.1 %reduce-scatter.5.cloned.1.call-done = f32[128,256]{0,1:T(8,128)} async-done(((f32[128,1024]{0,1:T(8,128)}), f32[128,256]{0,1:T(8,128)}) %reduce-scatter.5.cloned.1.call-update) | async-done | bytes 131088 | tf_op jit(solution)/shard_map/reduce_scatter | solution.py:51
  67.2 1.0 add_convert_fusion
  68.2 0.1 copy.15
  68.4 5.0 %all_gather.6 = bf16[512,128]{1,0:T(8,128)(2,1)} all-gather(bf16[256,128]{1,0:T(8,128)(2,1)S(1)} %pad_maximum_fusion), channel_id=1, replica_groups=mesh['zh'=4,'c'=2,'zl'=2,'x'=4,'y'=8] {'zl'}, dimensions={0}, use_global_device_ids=true | all-gather | bytes 196608 | tf_op jit(solution)/shard_map/all_gather | solution.py:58
  73.4 0.0 all-gather.2.cloned.1.call-update
  73.4 0.2 convolution_minimum_fusion.6
  73.7 0.2 convolution_minimum_fusion.5
  73.8 0.2 convolution_minimum_fusion.4
  74.0 0.2 convolution_minimum_fusion.3
  74.2 0.2 convolution_minimum_fusion.2
  74.4 0.2 convolution_minimum_fusion.1
  74.5 0.2 convolution_minimum_fusion
  74.7 0.2 fusion.4
  74.9 0.2 fusion.3
  75.2 0.1 copy.13
  75.3 0.1 reduce-window.8
  75.4 0.1 reduce
  75.5 0.6 fusion.14
  76.8 0.7 iota_minimum_fusion
  77.5 0.2 select_reduce_fusion
  77.6 0.7 fusion.15
  78.3 1.3 gather_fusion
  79.6 80.9 %all-gather.2.cloned.1.call-done.kva_ref.kvb_ref = bf16[16384,128]{1,0:T(8,128)(2,1)} async-done(((bf16[512,128]{1,0:T(8,128)(2,1)}), bf16[16384,128]{1,0:T(8,128)(2,1)}) %all-gather.2.cloned.1.call-update) | async-done | bytes 4194320 | tf_op jit(solution)/shard_map/all_gather | solution.py:59
  160.5 20.0 %shard_map.64 = bf16[128,1024]{1,0:T(8,128)(2,1)} custom-call(s32[64]{0:T(128)} %gather_fusion, s32[1]{0:T(128)} %bitcast.5.count_ref, bf16[128,1024]{1,0:T(8,128)(2,1)} %q_ref.1, bf16[16384,128]{1,0:T(8,128)(2,1)} %all-gather.2.cloned.1.call-done.kva_ref.kvb_ref, bf16[16384,128]{1,0:T(8,128)(2,1)} %all-gather.2.cloned.1.call-done.kva_ref.kvb_ref), custom_call_target="tpu_custom_call" | custom-call | tf_op jit(solution)/shard_map/pallas_call | solution.py:162
  (13 shorter events, 0.1 us)
Async XLA Ops:
  6.5 1.0 copy-start
  6.5 26.8 %reduce-scatter.3.cloned.1.call-start = ((), (), s32[]{:S(2)}) async-start(), calls=%async_computation.2 | async-start | bytes 1572864 | tf_op jit(solution)/shard_map/reduce_scatter | solution.py:50
  10.4 63.0 %copy-start.2 = (s32[64]{0:T(128)S(1)}, s32[64]{0:T(128)}, u32[]{:S(2)}) copy-start(s32[64]{0:T(128)} %param.10) | copy-start | bytes 772
  10.4 64.3 %copy-start.1 = (s32[64]{0:T(128)S(1)}, s32[64]{0:T(128)}, u32[]{:S(2)}) copy-start(s32[64]{0:T(128)} %param.11) | copy-start | bytes 772
  12.6 54.6 %reduce-scatter.5.cloned.1.call-start = ((), (), s32[]{:S(2)}) async-start(), calls=%async_computation.3 | async-start | bytes 655360 | tf_op jit(solution)/shard_map/reduce_scatter | solution.py:51
  33.3 127.2 %all-gather.2.cloned.1.call-start = ((), (), s32[]{:S(2)}) async-start(), calls=%async_computation.4 | async-start | bytes 4325376 | tf_op jit(solution)/shard_map/all_gather | solution.py:59
Sparse Core Ops, SparseCore 0:
  12.8 20.4 reduce-scatter.2
  36.1 31.0 reduce-scatter.4
  73.5 86.9 all-gather.1

commit v5 on v4

--- a/solution.py
+++ b/solution.py
@@ -43,12 +43,14 @@
     f_index = fsdp_index()
     n_zh = lax.axis_size("zh")
     n_c = lax.axis_size("c")
+    cols = kv_weight.shape[1]
+    per_head = cols // (n_zh * n_c)
     partial_sums = jnp.dot(hidden, kv_weight, preferred_element_type=jnp.float32)
-    cols = partial_sums.shape[1]
-    per_head = cols // (n_zh * n_c)
-    regrouped = partial_sums.reshape(tok_rows, n_zh, n_c, per_head).transpose(0, 2, 1, 3).reshape(tok_rows, cols)
-    half = lax.psum_scatter(regrouped, "c", scatter_dimension=1, tiled=True)
-    head_cols = lax.psum_scatter(half, "zh", scatter_dimension=1, tiled=True)
+    partial_sums = partial_sums.reshape(tok_rows, n_zh, n_c, per_head).transpose(2, 1, 0, 3)
+    from_core = lax.all_to_all(partial_sums, "c", 0, 0)
+    core_sums = jnp.sum(from_core, axis=0)
+    from_chip = lax.all_to_all(core_sums, "zh", 0, 0)
+    head_cols = jnp.sum(from_chip, axis=0)
     head_bias = lax.dynamic_slice_in_dim(kv_bias, f_index * 2 * HD, 2 * HD, 0)
     both_parts = (head_cols + head_bias).astype(jnp.bfloat16)
     kv_block = jnp.concatenate([both_parts[:, :HD], both_parts[:, HD:].T], axis=0)

time: 188 us -> 166 us (0.88)
  the two profiles are of different devices: /device:TPU:64 before, /device:TPU:6 now
where the time goes in v5:
time: 166 us; the launch traced here: 163 us
  waiting for transfers between devices  90.1 us (54%)
  Pallas kernels  23.2 us (14%)
  between operations  14.3 us (9%)
  blocking collectives  11.9 us (7%)
  starting transfers between devices  10.3 us (6%)
  local copies, waits for them, and re-layouts  5.38 us (3%)
  matrix products  4.55 us (3%)
  other arithmetic  2.95 us (2%)
    all_gather x1, waiting for transfers between devices, shards(): gathered = lax.all_gather(gathered, ('x', 'y'), axis=0, tiled=True)  76.7 us
    pallas_call x1, Pallas kernels, attention(): pl.pallas_call(kernel, grid_spec=grid_spec, out_shape=jax.ShapeDtypeStruc...  23.2 us
    all_to_all x1, waiting for transfers between devices, shards(): from_chip = lax.all_to_all(core_sums, 'zh', 0, 0)  13.3 us
    all_to_all x1, starting transfers between devices, shards(): from_chip = lax.all_to_all(core_sums, 'zh', 0, 0)  10.3 us
    all_gather x1, blocking collectives, shards(): gathered = lax.all_gather(kv_block, 'zl', axis=0, tiled=True)  7.3 us
    all_to_all x1, blocking collectives, shards(): from_core = lax.all_to_all(partial_sums, 'c', 0, 0)  4.58 us
  transfers between devices with their start and end apart: 2, of which 2 were waited for; matrix products, arithmetic and copies ran while one was open for 4% of the time, Pallas kernels for 0%

profile of v5, /device:TPU:6, one launch (start us, length us, event | category | flops | bytes accessed | tf_op | source)
XLA Modules:
  0.0 162.6 jit_solution(1363900938733146610)
XLA Ops:
  6.5 0.9 copy-done
  7.5 2.9 %fusion.17 = f32[128,2048]{1,0:T(8,128)S(1)} fusion(bf16[128,1024]{1,0:T(8,128)(2,1)S(1)} %copy-done, bf16[1024,2048]{1,0:T(8,128)(2,1)} %param.8), kind=kOutput, calls=%fused_computation.52 | convolution fusion | flops 536870912 | bytes 5505024 | tf_op jit(solution)/shard_map/dot_general | solution.py:48
  10.4 0.9 reshape.82
  11.3 0.3 copy.32
  11.6 4.6 %all_to_all.10 = f32[2,4,128,256]{3,1,2,0:T(4,128)S(1)} all-to-all(f32[2,4,128,256]{3,1,2,0:T(4,128)S(1)} %bitcast.37), channel_id=1, replica_groups=mesh['zh'=4,'c'=2,'zl'=2,'x'=4,'y'=8] {'c'}, dimensions={0} | all-to-all | bytes 2097152 | tf_op jit(solution)/shard_map/all_to_all | solution.py:50
  16.2 0.4 reduce_sum.41
  16.6 0.9 copy.25
  17.5 10.3 %all-to-all-start.1 = ((f32[4,128,256]{2,1,0:T(8,128)}), f32[4,128,256]{2,1,0:T(8,128)S(1)}, u32[]{:S(2)}, u32[]{:S(2)}) async-start(f32[4,128,256]{2,1,0:T(8,128)} %copy.25), calls=%async_computation.1 | async-start | bytes 1048576 | tf_op jit(solution)/shard_map/all_to_all | solution.py:52
  27.8 0.8 dynamic_slice.7
  28.6 13.3 %all-to-all-done.1 = f32[4,128,256]{2,1,0:T(8,128)S(1)} async-done(((f32[4,128,256]{2,1,0:T(8,128)}), f32[4,128,256]{2,1,0:T(8,128)S(1)}, u32[]{:S(2)}, u32[]{:S(2)}) %all-to-all-start.1) | async-done | bytes 524320 | tf_op jit(solution)/shard_map/all_to_all | solution.py:52
  42.0 0.1 add_convert_fusion
  42.1 0.1 copy.28
  42.2 7.3 %all_gather.6 = bf16[512,128]{1,0:T(8,128)(2,1)} all-gather(bf16[256,128]{1,0:T(8,128)(2,1)S(1)} %pad_maximum_fusion), channel_id=1, replica_groups=mesh['zh'=4,'c'=2,'zl'=2,'x'=4,'y'=8] {'zl'}, dimensions={0}, use_global_device_ids=true | all-gather | bytes 196608 | tf_op jit(solution)/shard_map/all_gather | solution.py:60
  49.6 0.2 convolution_minimum_fusion.6
  49.8 0.2 convolution_minimum_fusion.5
  50.0 0.2 convolution_minimum_fusion.4
  50.2 0.2 convolution_minimum_fusion.3
  50.3 0.2 convolution_minimum_fusion.2
  50.5 0.2 convolution_minimum_fusion.1
  50.7 0.2 convolution_minimum_fusion
  50.9 0.2 fusion.4
  51.1 0.2 fusion.3
  51.3 0.1 copy.22
  51.4 0.1 reduce-window.8
  51.5 0.1 reduce
  51.6 0.6 fusion.14
  53.0 0.7 iota_minimum_fusion
  53.6 0.2 select_reduce_fusion
  53.8 0.7 fusion.15
  54.5 1.3 gather_fusion
  55.8 76.7 %all-gather.2.cloned.1.call-done.kva_ref.kvb_ref = bf16[16384,128]{1,0:T(8,128)(2,1)} async-done(((bf16[512,128]{1,0:T(8,128)(2,1)}), bf16[16384,128]{1,0:T(8,128)(2,1)}) %all-gather.2.cloned.1.call-update) | async-done | bytes 4194320 | tf_op jit(solution)/shard_map/all_gather | solution.py:61
  132.5 23.2 %shard_map.64 = bf16[128,1024]{1,0:T(8,128)(2,1)} custom-call(s32[64]{0:T(128)} %gather_fusion, s32[1]{0:T(128)} %bitcast.5.count_ref, bf16[128,1024]{1,0:T(8,128)(2,1)} %q_ref.1, bf16[16384,128]{1,0:T(8,128)(2,1)} %all-gather.2.cloned.1.call-done.kva_ref.kvb_ref, bf16[16384,128]{1,0:T(8,128)(2,1)} %all-gather.2.cloned.1.call-done.kva_ref.kvb_ref), custom_call_target="tpu_custom_call" | custom-call | tf_op jit(solution)/shard_map/pallas_call | solution.py:164
  (14 shorter events, 0.2 us)
Async XLA Ops:
  6.5 1.0 copy-start
  11.6 38.0 %copy-start.2 = (s32[64]{0:T(128)S(1)}, s32[64]{0:T(128)}, u32[]{:S(2)}) copy-start(s32[64]{0:T(128)} %param.10) | copy-start | bytes 772
  11.6 39.3 %copy-start.1 = (s32[64]{0:T(128)S(1)}, s32[64]{0:T(128)}, u32[]{:S(2)}) copy-start(s32[64]{0:T(128)} %param.11) | copy-start | bytes 772
  17.5 24.4 %all-to-all-start.1 = ((f32[4,128,256]{2,1,0:T(8,128)}), f32[4,128,256]{2,1,0:T(8,128)S(1)}, u32[]{:S(2)}, u32[]{:S(2)}) async-start(f32[4,128,256]{2,1,0:T(8,128)} %copy.25), calls=%async_computation.1 | async-start | bytes 1048576 | tf_op jit(solution)/shard_map/all_to_all | solution.py:52
  27.8 104.7 %all-gather.2.cloned.1.call-start = ((), (), s32[]{:S(2)}) async-start(), calls=%async_computation.2 | async-start | bytes 4325376 | tf_op jit(solution)/shard_map/all_gather | solution.py:61
Sparse Core Ops, SparseCore 0:
  49.7 82.7 all-gather.1

commit v6 on v5

--- a/solution.py
+++ b/solution.py
@@ -33,6 +33,30 @@
 
 def fsdp_index():
     return lax.axis_index("zh") * lax.axis_size("c") + lax.axis_index("c")
+
+
+def shift(x, axis, n, step):
+    return lax.ppermute(x, axis, [(i, (i + step) % n) for i in range(n)])
+
+
+def ring_gather(x, axis, n):
+    if n == 1:
+        return x[None]
+    ahead = [x]
+    behind = [x]
+    for _ in range((n - 1) // 2):
+        ahead.append(shift(ahead[-1], axis, n, -1))
+        behind.append(shift(behind[-1], axis, n, 1))
+    middle = []
+    if n % 2 == 0:
+        if n == 2:
+            middle = [shift(x, axis, n, 1)]
+        else:
+            half = x.shape[0] // 2
+            far_behind = shift(behind[-1][:half], axis, n, 1)
+            far_ahead = shift(ahead[-1][half:], axis, n, -1)
+            middle = [jnp.concatenate([far_behind, far_ahead], axis=0)]
+    return jnp.stack(ahead + middle + behind[1:][::-1], axis=0)
 
 
 def shards(hidden, queries, kv_weight, kv_bias, parents, slot_block):
@@ -57,14 +81,18 @@
     visible = ancestry_table(parents, slot_block)
     own_slot = seq_index() * per_device
     own_visible = lax.dynamic_slice_in_dim(visible, own_slot, per_device, 0)
-    gathered = lax.all_gather(kv_block, "zl", axis=0, tiled=True)
-    gathered = lax.all_gather(gathered, ("x", "y"), axis=0, tiled=True)
     n_zl, n_x, n_y = lax.axis_size("zl"), lax.axis_size("x"), lax.axis_size("y")
+    pair = ring_gather(kv_block[None], "zl", n_zl)
+    plane = ring_gather(pair, "y", n_y)
+    gathered = ring_gather(plane, "x", n_x).reshape(-1, HD)
     slots = jnp.arange(visible.shape[1], dtype=jnp.int32)
     slot_zl = slots // (n_x * n_y)
     slot_x = (slots // n_y) % n_x
     slot_y = slots % n_y
-    physical = (slot_x * n_y + slot_y) * n_zl + slot_zl
+    rel_zl = (slot_zl - lax.axis_index("zl")) % n_zl
+    rel_x = (slot_x - lax.axis_index("x")) % n_x
+    rel_y = (slot_y - lax.axis_index("y")) % n_y
+    physical = (rel_x * n_y + rel_y) * n_zl + rel_zl
     others = (own_visible[0] > 0.5) & (slots != own_slot)
     count = jnp.sum(others.astype(jnp.int32)) + 1
     position = jnp.cumsum(others.astype(jnp.int32))

time: 166 us -> 164 us (0.988)
  the two profiles are of different devices: /device:TPU:6 before, /device:TPU:2 now
where the time goes in v6:
time: 164 us; the launch traced here: 163 us
  starting transfers between devices  57 us (35%)
  waiting for transfers between devices  51.6 us (31%)
  Pallas kernels  24 us (15%)
  local copies, waits for them, and re-layouts  13.3 us (8%)
  other arithmetic  6.48 us (4%)
  blocking collectives  4.58 us (3%)
  matrix products  4.55 us (3%)
    ppermute x13, starting transfers between devices, shift(): return lax.ppermute(x, axis, [(i, (i + step) % n) for i in range(n)])  46.7 us
    ppermute x13, waiting for transfers between devices, shift(): return lax.ppermute(x, axis, [(i, (i + step) % n) for i in range(n)])  38.9 us
    pallas_call x1, Pallas kernels, attention(): pl.pallas_call(kernel, grid_spec=grid_spec, out_shape=jax.ShapeDtypeStruc...  24 us
    all_to_all x1, waiting for transfers between devices, shards(): from_chip = lax.all_to_all(core_sums, 'zh', 0, 0)  12.7 us
    all_to_all x1, starting transfers between devices, shards(): from_chip = lax.all_to_all(core_sums, 'zh', 0, 0)  10.3 us
    another operation x2, local copies, waits for them, and re-layouts, ring_gather(): return jnp.stack(ahead + middle + behind[1:][::-1], axis=0)  6.24 us
    all_to_all x1, blocking collectives, shards(): from_core = lax.all_to_all(partial_sums, 'c', 0, 0)  4.58 us
    another operation x4, other arithmetic, ring_gather(): return jnp.stack(ahead + middle + behind[1:][::-1], axis=0)  3.6 us
  transfers between devices with their start and end apart: 14, of which 10 were waited for; matrix products, arithmetic and copies ran while one was open for 5% of the time, Pallas kernels for 0%

profile of v6, /device:TPU:2, one launch (start us, length us, event | category | flops | bytes accessed | tf_op | source)
XLA Modules:
  0.0 162.6 jit_solution(9952563524113772307)
XLA Ops:
  0.0 0.9 copy-done
  1.0 2.9 %fusion.27 = f32[128,2048]{1,0:T(8,128)S(1)} fusion(bf16[128,1024]{1,0:T(8,128)(2,1)S(1)} %copy-done, bf16[1024,2048]{1,0:T(8,128)(2,1)} %param.8), kind=kOutput, calls=%fused_computation.82 | convolution fusion | flops 536870912 | bytes 5505024 | tf_op jit(solution)/shard_map/dot_general | solution.py:72
  5.0 4.6 %all_to_all.10 = f32[2,4,128,256]{3,1,2,0:T(4,128)S(1)} all-to-all(f32[2,4,128,256]{3,1,2,0:T(4,128)S(1)} %bitcast.73), channel_id=1, replica_groups=mesh['zh'=4,'c'=2,'zl'=2,'x'=4,'y'=8] {'c'}, dimensions={0} | all-to-all | bytes 2097152 | tf_op jit(solution)/shard_map/all_to_all | solution.py:74
  10.1 0.9 copy.62
  11.0 10.3 %all-to-all-start.1 = ((f32[4,128,256]{2,1,0:T(8,128)}), f32[4,128,256]{2,1,0:T(8,128)S(1)}, u32[]{:S(2)}, u32[]{:S(2)}) async-start(f32[4,128,256]{2,1,0:T(8,128)} %copy.62), calls=%async_computation.1 | async-start | bytes 1048576 | tf_op jit(solution)/shard_map/all_to_all | solution.py:76
  22.6 12.7 %all-to-all-done.1 = f32[4,128,256]{2,1,0:T(8,128)S(1)} async-done(((f32[4,128,256]{2,1,0:T(8,128)}), f32[4,128,256]{2,1,0:T(8,128)S(1)}, u32[]{:S(2)}, u32[]{:S(2)}) %all-to-all-start.1) | async-done | bytes 524320 | tf_op jit(solution)/shard_map/all_to_all | solution.py:76
  35.5 6.2 %collective-permute-start = (bf16[1,256,128]{1,2,0:T(8,128)(2,1)S(1)}, bf16[1,256,128]{1,2,0:T(8,128)(2,1)S(1)}, u32[]{:S(2)}, u32[]{:S(2)}) collective-permute-start(bf16[1,256,128]{1,2,0:T(8,128)(2,1)S(1)} %get-tuple-element.10), channel_id=1, source_target_pairs={{0,32},{32,0},{1,33},{33,1},{2,34},{34,2},{3,35},{35,3},{4,36},{36... | collective-permute-start | bytes 196616 | tf_op jit(solution)/shard_map/ppermute | solution.py:39
  41.9 2.1 %collective-permute-done = bf16[1,256,128]{1,2,0:T(8,128)(2,1)S(1)} collective-permute-done((bf16[1,256,128]{1,2,0:T(8,128)(2,1)S(1)}, bf16[1,256,128]{1,2,0:T(8,128)(2,1)S(1)}, u32[]{:S(2)}, u32[]{:S(2)}) %collective-permute-start) | collective-permute-done | bytes 65568 | tf_op jit(solution)/shard_map/ppermute | solution.py:39
  44.0 5.4 %collective-permute-start.1 = (bf16[2,1,256,128]{2,3,0,1:T(8,128)(2,1)S(1)}, bf16[2,1,256,128]{2,3,0,1:T(8,128)(2,1)S(1)}, u32[]{:S(2)}, u32[]{:S(2)}) collective-permute-start(bf16[2,1,256,128]{2,3,0,1:T(8,128)(2,1)S(1)} %get-tuple-element.8), channel_id=1, source_target_pairs={{0,7},{1,0},{2,1},{3,2},{4,3},{5,4},{6,5},{7,6},{8,15},{9,8},{10,9... | collective-permute-start | bytes 393224 | tf_op jit(solution)/shard_map/ppermute | solution.py:39
  49.4 1.9 %collective-permute-start.4 = (bf16[2,1,256,128]{2,3,1,0:T(8,128)(2,1)S(1)}, bf16[2,1,256,128]{2,3,1,0:T(8,128)(2,1)S(1)}, u32[]{:S(2)}, u32[]{:S(2)}) collective-permute-start(bf16[2,1,256,128]{2,3,1,0:T(8,128)(2,1)S(1)} %get-tuple-element.7), channel_id=1, source_target_pairs={{0,1},{1,2},{2,3},{3,4},{4,5},{5,6},{6,7},{7,0},{8,9},{9,10},{10,1... | collective-permute-start | bytes 393224 | tf_op jit(solution)/shard_map/ppermute | solution.py:39
  51.5 5.9 %collective-permute-done.4 = bf16[2,1,256,128]{2,3,1,0:T(8,128)(2,1)S(1)} collective-permute-done((bf16[2,1,256,128]{2,3,1,0:T(8,128)(2,1)S(1)}, bf16[2,1,256,128]{2,3,1,0:T(8,128)(2,1)S(1)}, u32[]{:S(2)}, u32[]{:S(2)}) %collective-permute-start.4) | collective-permute-done | bytes 131104 | tf_op jit(solution)/shard_map/ppermute | solution.py:39
  57.5 1.9 %collective-permute-start.5 = (bf16[2,1,256,128]{2,3,0,1:T(8,128)(2,1)S(1)}, bf16[2,1,256,128]{2,3,0,1:T(8,128)(2,1)S(1)}, u32[]{:S(2)}, u32[]{:S(2)}) collective-permute-start(bf16[2,1,256,128]{2,3,0,1:T(8,128)(2,1)S(1)} %bitcast.81), channel_id=1, source_target_pairs={{0,1},{1,2},{2,3},{3,4},{4,5},{5,6},{6,7},{7,0},{8,9},{9,10},{10,1... | collective-permute-start | bytes 393224 | tf_op jit(solution)/shard_map/ppermute | solution.py:39
  59.4 5.1 %collective-permute-start.2 = (bf16[2,1,256,128]{2,3,0,1:T(8,128)(2,1)S(1)}, bf16[2,1,256,128]{2,3,0,1:T(8,128)(2,1)S(1)}, u32[]{:S(2)}, u32[]{:S(2)}) collective-permute-start(bf16[2,1,256,128]{2,3,0,1:T(8,128)(2,1)S(1)} %collective-permute-done.1), channel_id=1, source_target_pairs={{0,7},{1,0},{2,1},{3,2},{4,3},{5,4},{6,5},{7,6},{8,15},{9,8},{10,9... | collective-permute-start | bytes 393224 | tf_op jit(solution)/shard_map/ppermute | solution.py:39
  64.6 2.5 %collective-permute-done.2 = bf16[2,1,256,128]{2,3,0,1:T(8,128)(2,1)S(1)} collective-permute-done((bf16[2,1,256,128]{2,3,0,1:T(8,128)(2,1)S(1)}, bf16[2,1,256,128]{2,3,0,1:T(8,128)(2,1)S(1)}, u32[]{:S(2)}, u32[]{:S(2)}) %collective-permute-start.2) | collective-permute-done | bytes 131104 | tf_op jit(solution)/shard_map/ppermute | solution.py:39
  67.0 5.6 %collective-permute-start.3 = (bf16[2,1,256,128]{2,3,0,1:T(8,128)(2,1)S(1)}, bf16[2,1,256,128]{2,3,0,1:T(8,128)(2,1)S(1)}, u32[]{:S(2)}, u32[]{:S(2)}) collective-permute-start(bf16[2,1,256,128]{2,3,0,1:T(8,128)(2,1)S(1)} %collective-permute-done.2), channel_id=1, source_target_pairs={{0,7},{1,0},{2,1},{3,2},{4,3},{5,4},{6,5},{7,6},{8,15},{9,8},{10,9... | collective-permute-start | bytes 393224 | tf_op jit(solution)/shard_map/ppermute | solution.py:39
  72.6 1.9 %collective-permute-start.6 = (bf16[2,1,256,128]{2,3,0,1:T(8,128)(2,1)S(1)}, bf16[2,1,256,128]{2,3,0,1:T(8,128)(2,1)S(1)}, u32[]{:S(2)}, u32[]{:S(2)}) collective-permute-start(bf16[2,1,256,128]{2,3,0,1:T(8,128)(2,1)S(1)} %collective-permute-done.5), channel_id=1, source_target_pairs={{0,1},{1,2},{2,3},{3,4},{4,5},{5,6},{6,7},{7,0},{8,9},{9,10},{10,1... | collective-permute-start | bytes 393224 | tf_op jit(solution)/shard_map/ppermute | solution.py:39
  74.6 6.5 %collective-permute-done.6 = bf16[2,1,256,128]{2,3,0,1:T(8,128)(2,1)S(1)} collective-permute-done((bf16[2,1,256,128]{2,3,0,1:T(8,128)(2,1)S(1)}, bf16[2,1,256,128]{2,3,0,1:T(8,128)(2,1)S(1)}, u32[]{:S(2)}, u32[]{:S(2)}) %collective-permute-start.6) | collective-permute-done | bytes 131104 | tf_op jit(solution)/shard_map/ppermute | solution.py:39
  81.0 1.9 %collective-permute-start.7 = (bf16[1,1,256,128]{2,3,0,1:T(8,128)(2,1)S(1)}, bf16[1,1,256,128]{2,3,0,1:T(8,128)(2,1)S(1)}, u32[]{:S(2)}, u32[]{:S(2)}) collective-permute-start(bf16[1,1,256,128]{2,3,0,1:T(8,128)(2,1)S(1)} %slice.28), channel_id=1, source_target_pairs={{0,1},{1,2},{2,3},{3,4},{4,5},{5,6},{6,7},{7,0},{8,9},{9,10},{10,1... | collective-permute-start | bytes 196616 | tf_op jit(solution)/shard_map/ppermute | solution.py:39
  83.0 5.1 %collective-permute-start.8 = (bf16[1,1,256,128]{2,3,0,1:T(8,128)(2,1)S(1)}, bf16[1,1,256,128]{2,3,0,1:T(8,128)(2,1)S(1)}, u32[]{:S(2)}, u32[]{:S(2)}) collective-permute-start(bf16[1,1,256,128]{2,3,0,1:T(8,128)(2,1)S(1)} %slice.29), channel_id=1, source_target_pairs={{0,7},{1,0},{2,1},{3,2},{4,3},{5,4},{6,5},{7,6},{8,15},{9,8},{10,9... | collective-permute-start | bytes 196616 | tf_op jit(solution)/shard_map/ppermute | solution.py:39
  88.4 1.6 collective-permute-done.8
  90.1 3.4 %collective-permute-start.10 = (bf16[8,2,1,256,128]{3,4,1,2,0:T(8,128)(2,1)S(1)}, bf16[8,2,1,256,128]{3,4,1,2,0:T(8,128)(2,1)S(1)}, u32[]{:S(2)}, u32[]{:S(2)}) collective-permute-start(bf16[8,2,1,256,128]{3,4,1,2,0:T(8,128)(2,1)S(1)} %bitcast_dynamic-update-slice_fusion), channel_id=1, source_target_pairs={{0,8},{8,16},{16,24},{24,0},{1,9},{9,17},{17,25},{25,1},{2,10},{10... | collective-permute-start | bytes 3145736 | tf_op jit(solution)/shard_map/ppermute | solution.py:39
  93.5 2.4 %collective-permute-start.9 = (bf16[8,2,1,256,128]{3,4,1,0,2:T(8,128)(2,1)S(1)}, bf16[8,2,1,256,128]{3,4,1,0,2:T(8,128)(2,1)S(1)}, u32[]{:S(2)}, u32[]{:S(2)}) collective-permute-start(bf16[8,2,1,256,128]{3,4,1,0,2:T(8,128)(2,1)S(1)} %bitcast.77), channel_id=1, source_target_pairs={{0,24},{8,0},{16,8},{24,16},{1,25},{9,1},{17,9},{25,17},{2,26},{10... | collective-permute-start | bytes 3145736 | tf_op jit(solution)/shard_map/ppermute | solution.py:39
  99.0 13.3 %collective-permute-done.10 = bf16[8,2,1,256,128]{3,4,1,2,0:T(8,128)(2,1)S(1)} collective-permute-done((bf16[8,2,1,256,128]{3,4,1,2,0:T(8,128)(2,1)S(1)}, bf16[8,2,1,256,128]{3,4,1,2,0:T(8,128)(2,1)S(1)}, u32[]{:S(2)}, u32[]{:S(2)}) %collective-permute-start.10) | collective-permute-done | bytes 1048608 | tf_op jit(solution)/shard_map/ppermute | solution.py:39
  113.2 3.4 %collective-permute-start.11 = (bf16[4,2,1,256,128]{3,4,1,0,2:T(8,128)(2,1)}, bf16[4,2,1,256,128]{3,4,1,0,2:T(8,128)(2,1)}, u32[]{:S(2)}, u32[]{:S(2)}) collective-permute-start(bf16[4,2,1,256,128]{3,4,1,0,2:T(8,128)(2,1)} %slice.30), channel_id=1, source_target_pairs={{0,8},{8,16},{16,24},{24,0},{1,9},{9,17},{17,25},{25,1},{2,10},{10... | collective-permute-start | bytes 1572872 | tf_op jit(solution)/shard_map/ppermute | solution.py:39
  117.4 2.4 %collective-permute-start.12 = (bf16[4,2,1,256,128]{3,4,1,0,2:T(8,128)(2,1)}, bf16[4,2,1,256,128]{3,4,1,0,2:T(8,128)(2,1)}, u32[]{:S(2)}, u32[]{:S(2)}) collective-permute-start(bf16[4,2,1,256,128]{3,4,1,0,2:T(8,128)(2,1)} %slice.31), channel_id=1, source_target_pairs={{0,24},{8,0},{16,8},{24,16},{1,25},{9,1},{17,9},{25,17},{2,26},{10... | collective-permute-start | bytes 1572872 | tf_op jit(solution)/shard_map/ppermute | solution.py:39
  120.7 1.3 gather_fusion
  122.1 2.5 %collective-permute-done.11 = bf16[4,2,1,256,128]{3,4,1,0,2:T(8,128)(2,1)} collective-permute-done((bf16[4,2,1,256,128]{3,4,1,0,2:T(8,128)(2,1)}, bf16[4,2,1,256,128]{3,4,1,0,2:T(8,128)(2,1)}, u32[]{:S(2)}, u32[]{:S(2)}) %collective-permute-start.11) | collective-permute-done | bytes 524320 | tf_op jit(solution)/shard_map/ppermute | solution.py:39
  124.6 4.2 %collective-permute-done.12 = bf16[4,2,1,256,128]{3,4,1,0,2:T(8,128)(2,1)} collective-permute-done((bf16[4,2,1,256,128]{3,4,1,0,2:T(8,128)(2,1)}, bf16[4,2,1,256,128]{3,4,1,0,2:T(8,128)(2,1)}, u32[]{:S(2)}, u32[]{:S(2)}) %collective-permute-start.12) | collective-permute-done | bytes 524320 | tf_op jit(solution)/shard_map/ppermute | solution.py:39
  128.8 1.3 maximum_bitcast_fusion
  130.1 2.3 %pad_maximum_fusion = bf16[4,8,2,1,256,128]{4,5,2,1,3,0:T(8,128)(2,1)} fusion(bf16[1,8,2,1,256,128]{4,5,2,1,3,0:T(8,128)(2,1)S(1)} %bitcast.75, bf16[1,8,2,1,256,128]{4,5,2,1,3,0:T(8,128)(2,1)S(1)} %maximum_bitcast_fusion, bf16[1,8,2,1,256,128]{4,5,2,1,3,0:T(8,128)(2,1)S(1)} %bitcast.76, bf16[1,8,2,1,256,128]{4,5,2,1,3,0:T(8,128)(2,1)S(1)} %bitcast.78), kind=kLoop, calls=%fused_computation.1 | loop fusion | flops 6291456 | bytes 8388608 | tf_op jit(solution)/shard_map/stack | solution.py:59
  132.4 6.2 %copy.69 = bf16[4,8,2,1,256,128]{5,4,2,1,0,3:T(8,128)(2,1)} copy(bf16[4,8,2,1,256,128]{4,5,2,1,3,0:T(8,128)(2,1)} %pad_maximum_fusion) | data formatting | bytes 8388608 | tf_op jit(solution)/shard_map/stack | solution.py:59
  138.6 24.0 %shard_map.64 = bf16[128,1024]{1,0:T(8,128)(2,1)} custom-call(s32[64]{0:T(128)} %gather_fusion, s32[1]{0:T(128)} %bitcast.5.count_ref, bf16[128,1024]{1,0:T(8,128)(2,1)} %q_ref.1, bf16[16384,128]{1,0:T(8,128)(2,1)} %bitcast.71, bf16[16384,128]{1,0:T(8,128)(2,1)} %bitcast.72), custom_call_target="tpu_custom_call" | custom-call | tf_op jit(solution)/shard_map/pallas_call | solution.py:192
  (51 shorter events, 8.7 us)
Async XLA Ops:
  0.0 1.0 copy-start
  4.8 17.3 %copy-start.2 = (s32[64]{0:T(128)S(1)}, s32[64]{0:T(128)}, u32[]{:S(2)}) copy-start(s32[64]{0:T(128)} %param.10) | copy-start | bytes 772
  9.6 86.6 %copy-start.1 = (s32[64]{0:T(128)S(1)}, s32[64]{0:T(128)}, u32[]{:S(2)}) copy-start(s32[64]{0:T(128)} %param.11) | copy-start | bytes 772
  11.0 24.4 %all-to-all-start.1 = ((f32[4,128,256]{2,1,0:T(8,128)}), f32[4,128,256]{2,1,0:T(8,128)S(1)}, u32[]{:S(2)}, u32[]{:S(2)}) async-start(f32[4,128,256]{2,1,0:T(8,128)} %copy.62), calls=%async_computation.1 | async-start | bytes 1048576 | tf_op jit(solution)/shard_map/all_to_all | solution.py:76
  35.5 8.4 %collective-permute-start = (bf16[1,256,128]{1,2,0:T(8,128)(2,1)S(1)}, bf16[1,256,128]{1,2,0:T(8,128)(2,1)S(1)}, u32[]{:S(2)}, u32[]{:S(2)}) collective-permute-start(bf16[1,256,128]{1,2,0:T(8,128)(2,1)S(1)} %get-tuple-element.10), channel_id=1, source_target_pairs={{0,32},{32,0},{1,33},{33,1},{2,34},{34,2},{3,35},{35,3},{4,36},{36... | collective-permute-start | bytes 196616 | tf_op jit(solution)/shard_map/ppermute | solution.py:39
  44.0 15.4 %collective-permute-start.1 = (bf16[2,1,256,128]{2,3,0,1:T(8,128)(2,1)S(1)}, bf16[2,1,256,128]{2,3,0,1:T(8,128)(2,1)S(1)}, u32[]{:S(2)}, u32[]{:S(2)}) collective-permute-start(bf16[2,1,256,128]{2,3,0,1:T(8,128)(2,1)S(1)} %get-tuple-element.8), channel_id=1, source_target_pairs={{0,7},{1,0},{2,1},{3,2},{4,3},{5,4},{6,5},{7,6},{8,15},{9,8},{10,9... | collective-permute-start | bytes 393224 | tf_op jit(solution)/shard_map/ppermute | solution.py:39
  49.4 8.1 %collective-permute-start.4 = (bf16[2,1,256,128]{2,3,1,0:T(8,128)(2,1)S(1)}, bf16[2,1,256,128]{2,3,1,0:T(8,128)(2,1)S(1)}, u32[]{:S(2)}, u32[]{:S(2)}) collective-permute-start(bf16[2,1,256,128]{2,3,1,0:T(8,128)(2,1)S(1)} %get-tuple-element.7), channel_id=1, source_target_pairs={{0,1},{1,2},{2,3},{3,4},{4,5},{5,6},{6,7},{7,0},{8,9},{9,10},{10,1... | collective-permute-start | bytes 393224 | tf_op jit(solution)/shard_map/ppermute | solution.py:39
  57.5 15.1 %collective-permute-start.5 = (bf16[2,1,256,128]{2,3,0,1:T(8,128)(2,1)S(1)}, bf16[2,1,256,128]{2,3,0,1:T(8,128)(2,1)S(1)}, u32[]{:S(2)}, u32[]{:S(2)}) collective-permute-start(bf16[2,1,256,128]{2,3,0,1:T(8,128)(2,1)S(1)} %bitcast.81), channel_id=1, source_target_pairs={{0,1},{1,2},{2,3},{3,4},{4,5},{5,6},{6,7},{7,0},{8,9},{9,10},{10,1... | collective-permute-start | bytes 393224 | tf_op jit(solution)/shard_map/ppermute | solution.py:39
  59.4 7.6 %collective-permute-start.2 = (bf16[2,1,256,128]{2,3,0,1:T(8,128)(2,1)S(1)}, bf16[2,1,256,128]{2,3,0,1:T(8,128)(2,1)S(1)}, u32[]{:S(2)}, u32[]{:S(2)}) collective-permute-start(bf16[2,1,256,128]{2,3,0,1:T(8,128)(2,1)S(1)} %collective-permute-done.1), channel_id=1, source_target_pairs={{0,7},{1,0},{2,1},{3,2},{4,3},{5,4},{6,5},{7,6},{8,15},{9,8},{10,9... | collective-permute-start | bytes 393224 | tf_op jit(solution)/shard_map/ppermute | solution.py:39
  67.0 15.9 %collective-permute-start.3 = (bf16[2,1,256,128]{2,3,0,1:T(8,128)(2,1)S(1)}, bf16[2,1,256,128]{2,3,0,1:T(8,128)(2,1)S(1)}, u32[]{:S(2)}, u32[]{:S(2)}) collective-permute-start(bf16[2,1,256,128]{2,3,0,1:T(8,128)(2,1)S(1)} %collective-permute-done.2), channel_id=1, source_target_pairs={{0,7},{1,0},{2,1},{3,2},{4,3},{5,4},{6,5},{7,6},{8,15},{9,8},{10,9... | collective-permute-start | bytes 393224 | tf_op jit(solution)/shard_map/ppermute | solution.py:39
  72.6 8.4 %collective-permute-start.6 = (bf16[2,1,256,128]{2,3,0,1:T(8,128)(2,1)S(1)}, bf16[2,1,256,128]{2,3,0,1:T(8,128)(2,1)S(1)}, u32[]{:S(2)}, u32[]{:S(2)}) collective-permute-start(bf16[2,1,256,128]{2,3,0,1:T(8,128)(2,1)S(1)} %collective-permute-done.5), channel_id=1, source_target_pairs={{0,1},{1,2},{2,3},{3,4},{4,5},{5,6},{6,7},{7,0},{8,9},{9,10},{10,1... | collective-permute-start | bytes 393224 | tf_op jit(solution)/shard_map/ppermute | solution.py:39
  81.0 7.4 %collective-permute-start.7 = (bf16[1,1,256,128]{2,3,0,1:T(8,128)(2,1)S(1)}, bf16[1,1,256,128]{2,3,0,1:T(8,128)(2,1)S(1)}, u32[]{:S(2)}, u32[]{:S(2)}) collective-permute-start(bf16[1,1,256,128]{2,3,0,1:T(8,128)(2,1)S(1)} %slice.28), channel_id=1, source_target_pairs={{0,1},{1,2},{2,3},{3,4},{4,5},{5,6},{6,7},{7,0},{8,9},{9,10},{10,1... | collective-permute-start | bytes 196616 | tf_op jit(solution)/shard_map/ppermute | solution.py:39
  83.0 7.0 %collective-permute-start.8 = (bf16[1,1,256,128]{2,3,0,1:T(8,128)(2,1)S(1)}, bf16[1,1,256,128]{2,3,0,1:T(8,128)(2,1)S(1)}, u32[]{:S(2)}, u32[]{:S(2)}) collective-permute-start(bf16[1,1,256,128]{2,3,0,1:T(8,128)(2,1)S(1)} %slice.29), channel_id=1, source_target_pairs={{0,7},{1,0},{2,1},{3,2},{4,3},{5,4},{6,5},{7,6},{8,15},{9,8},{10,9... | collective-permute-start | bytes 196616 | tf_op jit(solution)/shard_map/ppermute | solution.py:39
  90.1 22.3 %collective-permute-start.10 = (bf16[8,2,1,256,128]{3,4,1,2,0:T(8,128)(2,1)S(1)}, bf16[8,2,1,256,128]{3,4,1,2,0:T(8,128)(2,1)S(1)}, u32[]{:S(2)}, u32[]{:S(2)}) collective-permute-start(bf16[8,2,1,256,128]{3,4,1,2,0:T(8,128)(2,1)S(1)} %bitcast_dynamic-update-slice_fusion), channel_id=1, source_target_pairs={{0,8},{8,16},{16,24},{24,0},{1,9},{9,17},{17,25},{25,1},{2,10},{10... | collective-permute-start | bytes 3145736 | tf_op jit(solution)/shard_map/ppermute | solution.py:39
  93.5 23.1 %collective-permute-start.9 = (bf16[8,2,1,256,128]{3,4,1,0,2:T(8,128)(2,1)S(1)}, bf16[8,2,1,256,128]{3,4,1,0,2:T(8,128)(2,1)S(1)}, u32[]{:S(2)}, u32[]{:S(2)}) collective-permute-start(bf16[8,2,1,256,128]{3,4,1,0,2:T(8,128)(2,1)S(1)} %bitcast.77), channel_id=1, source_target_pairs={{0,24},{8,0},{16,8},{24,16},{1,25},{9,1},{17,9},{25,17},{2,26},{10... | collective-permute-start | bytes 3145736 | tf_op jit(solution)/shard_map/ppermute | solution.py:39
  113.2 11.4 %collective-permute-start.11 = (bf16[4,2,1,256,128]{3,4,1,0,2:T(8,128)(2,1)}, bf16[4,2,1,256,128]{3,4,1,0,2:T(8,128)(2,1)}, u32[]{:S(2)}, u32[]{:S(2)}) collective-permute-start(bf16[4,2,1,256,128]{3,4,1,0,2:T(8,128)(2,1)} %slice.30), channel_id=1, source_target_pairs={{0,8},{8,16},{16,24},{24,0},{1,9},{9,17},{17,25},{25,1},{2,10},{10... | collective-permute-start | bytes 1572872 | tf_op jit(solution)/shard_map/ppermute | solution.py:39
  117.4 11.4 %collective-permute-start.12 = (bf16[4,2,1,256,128]{3,4,1,0,2:T(8,128)(2,1)}, bf16[4,2,1,256,128]{3,4,1,0,2:T(8,128)(2,1)}, u32[]{:S(2)}, u32[]{:S(2)}) collective-permute-start(bf16[4,2,1,256,128]{3,4,1,0,2:T(8,128)(2,1)} %slice.31), channel_id=1, source_target_pairs={{0,24},{8,0},{16,8},{24,16},{1,25},{9,1},{17,9},{25,17},{2,26},{10... | collective-permute-start | bytes 1572872 | tf_op jit(solution)/shard_map/ppermute | solution.py:39

commit v7 on v5

--- a/solution.py
+++ b/solution.py
@@ -57,14 +57,15 @@
     visible = ancestry_table(parents, slot_block)
     own_slot = seq_index() * per_device
     own_visible = lax.dynamic_slice_in_dim(visible, own_slot, per_device, 0)
-    gathered = lax.all_gather(kv_block, "zl", axis=0, tiled=True)
-    gathered = lax.all_gather(gathered, ("x", "y"), axis=0, tiled=True)
     n_zl, n_x, n_y = lax.axis_size("zl"), lax.axis_size("x"), lax.axis_size("y")
+    spread = jnp.broadcast_to(kv_block[None], (n_zl * n_y,) + kv_block.shape)
+    plane = lax.all_to_all(spread, ("zl", "y"), 0, 0)
+    gathered = lax.all_gather(plane, "x", axis=0, tiled=True).reshape(-1, HD)
     slots = jnp.arange(visible.shape[1], dtype=jnp.int32)
     slot_zl = slots // (n_x * n_y)
     slot_x = (slots // n_y) % n_x
     slot_y = slots % n_y
-    physical = (slot_x * n_y + slot_y) * n_zl + slot_zl
+    physical = (slot_x * n_zl + slot_zl) * n_y + slot_y
     others = (own_visible[0] > 0.5) & (slots != own_slot)
     count = jnp.sum(others.astype(jnp.int32)) + 1
     position = jnp.cumsum(others.astype(jnp.int32))

time: 166 us -> 159 us (0.958)
  the two profiles are of different devices: /device:TPU:6 before, /device:TPU:32 now
where the time goes in v7:
time: 159 us; the launch traced here: 158 us
  waiting for transfers between devices  58.2 us (37%)
  blocking collectives  38.3 us (24%)
  Pallas kernels  24 us (15%)
  between operations  14.3 us (9%)
  starting transfers between devices  10.3 us (6%)
  local copies, waits for them, and re-layouts  5.6 us (4%)
  matrix products  4.55 us (3%)
  other arithmetic  2.87 us (2%)
    all_gather x1, waiting for transfers between devices, shards(): gathered = lax.all_gather(plane, 'x', axis=0, tiled=True).reshape(-1, HD)  44.9 us
    all_to_all x1, blocking collectives, shards(): plane = lax.all_to_all(spread, ('zl', 'y'), 0, 0)  33.7 us
    pallas_call x1, Pallas kernels, attention(): pl.pallas_call(kernel, grid_spec=grid_spec, out_shape=jax.ShapeDtypeStruc...  24 us
    all_to_all x1, waiting for transfers between devices, shards(): from_chip = lax.all_to_all(core_sums, 'zh', 0, 0)  13.3 us
    all_to_all x1, starting transfers between devices, shards(): from_chip = lax.all_to_all(core_sums, 'zh', 0, 0)  10.3 us
    all_to_all x1, blocking collectives, shards(): from_core = lax.all_to_all(partial_sums, 'c', 0, 0)  4.58 us
  transfers between devices with their start and end apart: 2, of which 2 were waited for; matrix products, arithmetic and copies ran while one was open for 4% of the time, Pallas kernels for 0%

profile of v7, /device:TPU:32, one launch (start us, length us, event | category | flops | bytes accessed | tf_op | source)
XLA Modules:
  0.0 158.0 jit_solution(9070093880870320708)
XLA Ops:
  6.5 0.9 copy-done
  7.5 2.9 %fusion.17 = f32[128,2048]{1,0:T(8,128)S(1)} fusion(bf16[128,1024]{1,0:T(8,128)(2,1)S(1)} %copy-done, bf16[1024,2048]{1,0:T(8,128)(2,1)} %param.8), kind=kOutput, calls=%fused_computation.52 | convolution fusion | flops 536870912 | bytes 5505024 | tf_op jit(solution)/shard_map/dot_general | solution.py:48
  10.4 0.9 reshape.86
  11.3 0.3 copy.33
  11.6 4.6 %all_to_all.15 = f32[2,4,128,256]{3,1,2,0:T(4,128)S(1)} all-to-all(f32[2,4,128,256]{3,1,2,0:T(4,128)S(1)} %bitcast.40), channel_id=1, replica_groups=mesh['zh'=4,'c'=2,'zl'=2,'x'=4,'y'=8] {'c'}, dimensions={0} | all-to-all | bytes 2097152 | tf_op jit(solution)/shard_map/all_to_all | solution.py:50
  16.1 0.4 reduce_sum.41
  16.6 0.9 copy.25
  17.5 10.3 %all-to-all-start.1 = ((f32[4,128,256]{2,1,0:T(8,128)}), f32[4,128,256]{2,1,0:T(8,128)S(1)}, u32[]{:S(2)}, u32[]{:S(2)}) async-start(f32[4,128,256]{2,1,0:T(8,128)} %copy.25), calls=%async_computation.1 | async-start | bytes 1048576 | tf_op jit(solution)/shard_map/all_to_all | solution.py:52
  27.8 0.8 dynamic_slice.7
  28.6 13.3 %all-to-all-done.1 = f32[4,128,256]{2,1,0:T(8,128)S(1)} async-done(((f32[4,128,256]{2,1,0:T(8,128)}), f32[4,128,256]{2,1,0:T(8,128)S(1)}, u32[]{:S(2)}, u32[]{:S(2)}) %all-to-all-start.1) | async-done | bytes 524320 | tf_op jit(solution)/shard_map/all_to_all | solution.py:52
  41.9 0.1 copy.31
  42.1 0.1 copy.28
  42.2 0.2 broadcast_in_dim.10
  42.4 33.7 %all_to_all.16 = bf16[16,256,128]{2,1,0:T(8,128)(2,1)} all-to-all(bf16[16,256,128]{2,1,0:T(8,128)(2,1)S(1)} %broadcast_in_dim.10), channel_id=1, replica_groups=mesh['zh'=4,'c'=2,'zl'=2,'x'=4,'y'=8] {'zl','y'}, dimensions={0} | all-to-all | bytes 2097152 | tf_op jit(solution)/shard_map/all_to_all | solution.py:62
  76.1 0.2 convolution_minimum_fusion.6
  76.4 0.2 convolution_minimum_fusion.5
  76.5 0.2 convolution_minimum_fusion.4
  76.7 0.2 convolution_minimum_fusion.3
  76.9 0.2 convolution_minimum_fusion.2
  77.1 0.2 convolution_minimum_fusion.1
  77.2 0.2 convolution_minimum_fusion
  77.4 0.2 fusion.4
  77.6 0.2 fusion.3
  77.9 0.1 copy.22
  78.1 0.1 reduce
  78.2 0.6 fusion.14
  79.5 0.7 iota_minimum_fusion
  80.2 0.2 select_reduce_fusion
  80.3 0.7 fusion.15
  81.0 1.3 gather_fusion
  82.3 44.9 %all-gather.2.cloned.1.call-done = bf16[64,256,128]{2,1,0:T(8,128)(2,1)} async-done(((bf16[16,256,128]{2,1,0:T(8,128)(2,1)}), bf16[64,256,128]{2,1,0:T(8,128)(2,1)}) %all-gather.2.cloned.1.call-update) | async-done | bytes 4194320 | tf_op jit(solution)/shard_map/all_gather | solution.py:63
  127.2 24.0 %shard_map.64 = bf16[128,1024]{1,0:T(8,128)(2,1)} custom-call(s32[64]{0:T(128)} %gather_fusion, s32[1]{0:T(128)} %bitcast.5.count_ref, bf16[128,1024]{1,0:T(8,128)(2,1)} %q_ref.1, bf16[16384,128]{1,0:T(8,128)(2,1)} %bitcast.38, bf16[16384,128]{1,0:T(8,128)(2,1)} %bitcast.39), custom_call_target="tpu_custom_call" | custom-call | tf_op jit(solution)/shard_map/pallas_call | solution.py:165
  (15 shorter events, 0.2 us)
Async XLA Ops:
  6.5 1.0 copy-start
  16.6 59.5 %copy-start.2 = (s32[64]{0:T(128)S(1)}, s32[64]{0:T(128)}, u32[]{:S(2)}) copy-start(s32[64]{0:T(128)} %param.10) | copy-start | bytes 772
  16.6 60.8 %copy-start.1 = (s32[64]{0:T(128)S(1)}, s32[64]{0:T(128)}, u32[]{:S(2)}) copy-start(s32[64]{0:T(128)} %param.11) | copy-start | bytes 772
  17.5 24.4 %all-to-all-start.1 = ((f32[4,128,256]{2,1,0:T(8,128)}), f32[4,128,256]{2,1,0:T(8,128)S(1)}, u32[]{:S(2)}, u32[]{:S(2)}) async-start(f32[4,128,256]{2,1,0:T(8,128)} %copy.25), calls=%async_computation.1 | async-start | bytes 1048576 | tf_op jit(solution)/shard_map/all_to_all | solution.py:52
  27.8 99.4 %all-gather.2.cloned.1.call-start = ((), (), s32[]{:S(2)}) async-start(), calls=%async_computation.3 | async-start | bytes 5242880 | tf_op jit(solution)/shard_map/all_gather | solution.py:63
Sparse Core Ops, SparseCore 0:
  76.2 50.8 all-gather.1

commit v8 on v5

--- a/solution.py
+++ b/solution.py
@@ -57,30 +57,38 @@
     visible = ancestry_table(parents, slot_block)
     own_slot = seq_index() * per_device
     own_visible = lax.dynamic_slice_in_dim(visible, own_slot, per_device, 0)
-    gathered = lax.all_gather(kv_block, "zl", axis=0, tiled=True)
-    gathered = lax.all_gather(gathered, ("x", "y"), axis=0, tiled=True)
     n_zl, n_x, n_y = lax.axis_size("zl"), lax.axis_size("x"), lax.axis_size("y")
+    plane_size = n_zl * n_y
+    keys = both_parts[:, :HD]
+    values_t = both_parts[:, HD:].T
+    key_plane = lax.all_to_all(jnp.broadcast_to(keys[None], (plane_size,) + keys.shape), ("zl", "y"), 0, 0)
+    key_all = lax.all_gather(key_plane, "x", axis=0, tiled=True).reshape(-1, HD)
+    value_row = lax.all_gather(values_t[None], "x", axis=0, tiled=True)
+    value_all = lax.all_to_all(
+        jnp.broadcast_to(value_row[None], (plane_size,) + value_row.shape), ("zl", "y"), 0, 0
+    ).reshape(-1, HD)
     slots = jnp.arange(visible.shape[1], dtype=jnp.int32)
     slot_zl = slots // (n_x * n_y)
     slot_x = (slots // n_y) % n_x
     slot_y = slots % n_y
-    physical = (slot_x * n_y + slot_y) * n_zl + slot_zl
+    key_physical = (slot_x * n_zl + slot_zl) * n_y + slot_y
+    value_physical = (slot_zl * n_y + slot_y) * n_x + slot_x
     others = (own_visible[0] > 0.5) & (slots != own_slot)
     count = jnp.sum(others.astype(jnp.int32)) + 1
     position = jnp.cumsum(others.astype(jnp.int32))
     wanted = jnp.minimum(slots, count - 1)
     hit = others[None, :] & (position[None, :] == wanted[:, None])
     order = jnp.where(wanted == 0, own_slot, jnp.sum(jnp.where(hit, slots[None, :], 0), axis=1))
-    order_physical = physical[order].astype(jnp.int32)
-    return attention(order_physical, count.reshape(1), queries, gathered, head_count, score_scale)
+    order_physical = jnp.stack([key_physical[order], value_physical[order]]).astype(jnp.int32)
+    return attention(order_physical, count.reshape(1), queries, key_all, value_all, head_count, score_scale)
 
 
-def attention(order_physical, count, queries, kv, head_count, score_scale):
+def attention(order_physical, count, queries, key_all, value_all, head_count, score_scale):
     tok_rows = queries.shape[0]
     rows = tok_rows * head_count
-    steps = order_physical.shape[0] // 2
+    steps = order_physical.shape[1] // 2
 
-    def kernel(order_ref, count_ref, q_ref, kva_ref, kvb_ref, o_ref, q_scr, m_scr, l_scr, acc_scr):
+    def kernel(order_ref, count_ref, q_ref, ka_ref, kb_ref, va_ref, vb_ref, o_ref, q_scr, m_scr, l_scr, acc_scr):
         i = pl.program_id(0)
 
         @pl.when(i == 0)
@@ -92,8 +100,8 @@
             l_scr[...] = jnp.zeros(l_scr.shape, jnp.float32)
             acc_scr[...] = jnp.zeros(acc_scr.shape, jnp.float32)
 
-        def scores_of(kv_ref, causal):
-            s_t = jnp.dot(kv_ref[:BLOCK, :], q_scr[...], preferred_element_type=jnp.float32) * score_scale
+        def scores_of(k_ref, causal):
+            s_t = jnp.dot(k_ref[...], q_scr[...], preferred_element_type=jnp.float32) * score_scale
             if causal:
                 key = lax.broadcasted_iota(jnp.int32, (BLOCK, rows), 0)
                 tok = lax.broadcasted_iota(jnp.int32, (BLOCK, rows), 1) % tok_rows
@@ -101,9 +109,9 @@
             return s_t
 
         def step(first_causal, with_second):
-            parts = [(scores_of(kva_ref, first_causal), kva_ref)]
+            parts = [(scores_of(ka_ref, first_causal), va_ref)]
             if with_second:
-                parts.append((scores_of(kvb_ref, False), kvb_ref))
+                parts.append((scores_of(kb_ref, False), vb_ref))
             m_old = m_scr[...]
             m_new = m_old
             for s_t, _ in parts:
@@ -114,7 +122,7 @@
             for s_t, ref in parts:
                 expo = jnp.exp(s_t - m_new)
                 l_new = l_new + jnp.sum(expo, axis=0, keepdims=True)
-                acc_new = acc_new + jnp.dot(ref[BLOCK:, :], expo.astype(jnp.bfloat16), preferred_element_type=jnp.float32)
+                acc_new = acc_new + jnp.dot(ref[...], expo.astype(jnp.bfloat16), preferred_element_type=jnp.float32)
             l_scr[...] = l_new
             acc_scr[...] = acc_new
             m_scr[...] = m_new
@@ -150,8 +158,10 @@
         grid=(steps,),
         in_specs=[
             pl.BlockSpec((tok_rows, head_count * HD), lambda i, o, c: (0, 0)),
-            pl.BlockSpec((2 * BLOCK, HD), lambda i, o, c: (o[2 * i], 0)),
-            pl.BlockSpec((2 * BLOCK, HD), lambda i, o, c: (o[2 * i + 1], 0)),
+            pl.BlockSpec((BLOCK, HD), lambda i, o, c: (o[0, 2 * i], 0)),
+            pl.BlockSpec((BLOCK, HD), lambda i, o, c: (o[0, 2 * i + 1], 0)),
+            pl.BlockSpec((HD, BLOCK), lambda i, o, c: (o[1, 2 * i], 0)),
+            pl.BlockSpec((HD, BLOCK), lambda i, o, c: (o[1, 2 * i + 1], 0)),
         ],
         out_specs=pl.BlockSpec((tok_rows, head_count * HD), lambda i, o, c: (0, 0)),
         scratch_shapes=[
@@ -166,7 +176,7 @@
         grid_spec=grid_spec,
         out_shape=jax.ShapeDtypeStruct((tok_rows, head_count * HD), jnp.bfloat16),
         compiler_params=pltpu.CompilerParams(dimension_semantics=("arbitrary",)),
-    )(order_physical, count, queries, kv, kv)
+    )(order_physical, count, queries, key_all, key_all, value_all, value_all)
 
 
 def solution(mesh):

time: 166 us -> 155 us (0.934)
  waiting for transfers between devices: 90.1 us -> 58.2 us
  starting transfers between devices: 10.3 us -> 26.6 us
  local copies, waits for them, and re-layouts: 5.38 us -> 9.53 us
  blocking collectives: 11.9 us -> 15 us
  Pallas kernels: 23.2 us -> 21 us
    all_gather x1, waiting for transfers between devices: 76.7 us -> 0.01 us  [shards(): key_all = lax.all_gather(key_plane, 'x', axis=0, tiled=True).reshape(-1, HD)]
    all_to_all x0 -> x2, waiting for transfers between devices: none -> 44.3 us  [the longest x1 40.5 us: shards(): lax.all_to_all(jnp.broadcast_to(value_row[None], (plane_size,) + value_ro...]
    all_to_all x0 -> x2, starting transfers between devices: none -> 16.2 us  [the longest x1 11.1 us: shards(): lax.all_to_all(jnp.broadcast_to(keys[None], (plane_size,) + keys.shape),...]
    all_gather x1, blocking collectives: 7.3 us -> 10.4 us  [shards(): value_row = lax.all_gather(values_t[None], 'x', axis=0, tiled=True)]
    broadcast_in_dim x0 -> x2, local copies, waits for them, and re-layouts: none -> 2.69 us  [the longest x1 1.8 us: shards(): jnp.broadcast_to(value_row[None], (plane_size,) + value_row.shape)]
    pallas_call x1, Pallas kernels: 23.2 us -> 21 us  [attention(): pl.pallas_call(kernel, grid_spec=grid_spec, out_shape=jax.ShapeDtypeStruc...]
  transfers between devices with their start and end apart: 2 -> 4, of which waited for: 2 -> 3; matrix products, arithmetic and copies ran while one was open for 4% -> 5% of each run, Pallas kernels for 0% -> 0%
where the time goes in v8:
time: 155 us; the launch traced here: 153 us
  waiting for transfers between devices  58.2 us (38%)
  starting transfers between devices  26.6 us (17%)
  Pallas kernels  21 us (14%)
  blocking collectives  15 us (10%)
  between operations  14.3 us (9%)
  local copies, waits for them, and re-layouts  9.53 us (6%)
  matrix products  4.54 us (3%)
  other arithmetic  3.42 us (2%)
    all_to_all x1, waiting for transfers between devices, shards(): lax.all_to_all(jnp.broadcast_to(value_row[None], (plane_size,) + value_ro...  40.5 us
    pallas_call x1, Pallas kernels, attention(): pl.pallas_call(kernel, grid_spec=grid_spec, out_shape=jax.ShapeDtypeStruc...  21 us
    all_to_all x1, waiting for transfers between devices, shards(): from_chip = lax.all_to_all(core_sums, 'zh', 0, 0)  13.3 us
    all_to_all x1, starting transfers between devices, shards(): lax.all_to_all(jnp.broadcast_to(keys[None], (plane_size,) + keys.shape),...  11.1 us
    all_gather x1, blocking collectives, shards(): value_row = lax.all_gather(values_t[None], 'x', axis=0, tiled=True)  10.4 us
    all_to_all x1, starting transfers between devices, shards(): from_chip = lax.all_to_all(core_sums, 'zh', 0, 0)  10.3 us
    all_to_all x1, starting transfers between devices, shards(): lax.all_to_all(jnp.broadcast_to(value_row[None], (plane_size,) + value_ro...  5.14 us
    all_to_all x1, blocking collectives, shards(): from_core = lax.all_to_all(partial_sums, 'c', 0, 0)  4.58 us
  transfers between devices with their start and end apart: 4, of which 3 were waited for; matrix products, arithmetic and copies ran while one was open for 5% of the time, Pallas kernels for 0%

profile of v8, /device:TPU:6, one launch (start us, length us, event | category | flops | bytes accessed | tf_op | source)
XLA Modules:
  0.0 152.6 jit_solution(16777120583596066692)
XLA Ops:
  6.5 0.9 copy-done
  7.5 2.9 %fusion.12 = f32[128,2048]{1,0:T(8,128)S(1)} fusion(bf16[128,1024]{1,0:T(8,128)(2,1)S(1)} %copy-done, bf16[1024,2048]{1,0:T(8,128)(2,1)} %param.8), kind=kOutput, calls=%fused_computation.50 | convolution fusion | flops 536870912 | bytes 5505024 | tf_op jit(solution)/shard_map/dot_general | solution.py:48
  10.4 0.9 reshape.90
  11.3 0.3 copy.28
  11.6 4.6 %all_to_all.20 = f32[2,4,128,256]{3,1,2,0:T(4,128)S(1)} all-to-all(f32[2,4,128,256]{3,1,2,0:T(4,128)S(1)} %bitcast.46), channel_id=1, replica_groups=mesh['zh'=4,'c'=2,'zl'=2,'x'=4,'y'=8] {'c'}, dimensions={0} | all-to-all | bytes 2097152 | tf_op jit(solution)/shard_map/all_to_all | solution.py:50
  16.1 0.4 reduce_sum.41
  16.6 0.9 copy.23
  17.5 10.3 %all-to-all-start.1 = ((f32[4,128,256]{2,1,0:T(8,128)}), f32[4,128,256]{2,1,0:T(8,128)S(1)}, u32[]{:S(2)}, u32[]{:S(2)}) async-start(f32[4,128,256]{2,1,0:T(8,128)} %copy.23), calls=%async_computation.1 | async-start | bytes 1048576 | tf_op jit(solution)/shard_map/all_to_all | solution.py:52
  27.8 0.8 dynamic_slice.7
  28.5 13.3 %all-to-all-done.1 = f32[4,128,256]{2,1,0:T(8,128)S(1)} async-done(((f32[4,128,256]{2,1,0:T(8,128)}), f32[4,128,256]{2,1,0:T(8,128)S(1)}, u32[]{:S(2)}, u32[]{:S(2)}) %all-to-all-start.1) | async-done | bytes 524320 | tf_op jit(solution)/shard_map/all_to_all | solution.py:52
  41.9 0.9 broadcast_in_dim.14
  42.8 11.1 %all-to-all-start.2 = ((bf16[16,128,128]{2,1,0:T(8,128)(2,1)}), bf16[16,128,128]{2,1,0:T(8,128)(2,1)S(1)}, u32[]{:S(2)}, u32[]{:S(2)}) async-start(bf16[16,128,128]{2,1,0:T(8,128)(2,1)} %broadcast_in_dim.14), calls=%async_computation.2 | async-start | bytes 1048576 | tf_op jit(solution)/shard_map/all_to_all | solution.py:64
  53.9 10.4 %all-gather = bf16[512,128]{0,1:T(8,128)(2,1)S(1)} all-gather(bf16[128,128]{0,1:T(8,128)(2,1)S(1)} %get-tuple-element.7), channel_id=2, replica_groups=mesh['zh'=4,'c'=2,'zl'=2,'x'=4,'y'=8] {'x'}, dimensions={0}, use_global_device_ids=true | all-gather | bytes 163840 | tf_op jit(solution)/shard_map/all_gather | solution.py:66
  64.5 3.8 %all-to-all-done.2 = bf16[16,128,128]{2,1,0:T(8,128)(2,1)S(1)} async-done(((bf16[16,128,128]{2,1,0:T(8,128)(2,1)}), bf16[16,128,128]{2,1,0:T(8,128)(2,1)S(1)}, u32[]{:S(2)}, u32[]{:S(2)}) %all-to-all-start.2) | async-done | bytes 524320 | tf_op jit(solution)/shard_map/all_to_all | solution.py:64
  68.3 1.8 %broadcast_in_dim.16 = bf16[16,4,128,128]{3,2,1,0:T(8,128)(2,1)} broadcast(bf16[4,128,128]{2,1,0:T(8,128)(2,1)S(1)} %bitcast.47), dimensions={1,2,3} | broadcast | bytes 2228224 | tf_op jit(solution)/shard_map/broadcast_in_dim | solution.py:68
  70.1 5.1 %all-to-all-start.3 = ((bf16[16,4,128,128]{3,2,1,0:T(8,128)(2,1)}), bf16[16,4,128,128]{3,2,1,0:T(8,128)(2,1)S(1)}, u32[]{:S(2)}, u32[]{:S(2)}) async-start(bf16[16,4,128,128]{3,2,1,0:T(8,128)(2,1)} %broadcast_in_dim.16), calls=%async_computation.3 | async-start | bytes 4194304 | tf_op jit(solution)/shard_map/all_to_all | solution.py:67
  75.3 0.7 all-gather.3.cloned.1.call-update
  76.0 0.2 convolution_minimum_fusion.6
  76.9 0.2 convolution_minimum_fusion.1
  77.1 0.2 convolution_minimum_fusion
  77.2 0.2 fusion.4
  77.5 0.2 fusion.3
  78.0 0.6 fusion.10
  78.7 0.6 iota_minimum_fusion
  79.3 0.2 select_reduce_fusion
  79.5 0.7 fusion.11
  80.2 0.8 gather_fusion
  81.0 0.8 gather_fusion.1
  82.4 0.6 pad_add_fusion.order_ref
  83.0 40.5 %all-to-all-done.3 = bf16[16,4,128,128]{3,2,1,0:T(8,128)(2,1)S(1)} async-done(((bf16[16,4,128,128]{3,2,1,0:T(8,128)(2,1)}), bf16[16,4,128,128]{3,2,1,0:T(8,128)(2,1)S(1)}, u32[]{:S(2)}, u32[]{:S(2)}) %all-to-all-start.3) | async-done | bytes 2097184 | tf_op jit(solution)/shard_map/all_to_all | solution.py:67
  123.4 1.3 copy-done.1
  124.7 21.0 %shard_map.64 = bf16[128,1024]{1,0:T(8,128)(2,1)} custom-call(s32[2,64]{1,0:T(2,128)} %pad_add_fusion.order_ref, s32[1]{0:T(128)} %bitcast.7.count_ref, bf16[128,1024]{1,0:T(8,128)(2,1)} %q_ref.1, bf16[8192,128]{1,0:T(8,128)(2,1)} %bitcast.44, bf16[8192,128]{1,0:T(8,128)(2,1)} %bitcast.45, bf16[8192,128]{1,0:T(8,128)(2,1)} %bitcast.42, ...), custom_call_target="tpu_custom_call" | custom-call | tf_op jit(solution)/shard_map/pallas_call | solution.py:174
  (25 shorter events, 1.2 us)
Async XLA Ops:
  6.5 1.0 copy-start
  17.5 24.4 %all-to-all-start.1 = ((f32[4,128,256]{2,1,0:T(8,128)}), f32[4,128,256]{2,1,0:T(8,128)S(1)}, u32[]{:S(2)}, u32[]{:S(2)}) async-start(f32[4,128,256]{2,1,0:T(8,128)} %copy.23), calls=%async_computation.1 | async-start | bytes 1048576 | tf_op jit(solution)/shard_map/all_to_all | solution.py:52
  42.8 33.2 %copy-start.4 = (s32[64]{0:T(128)S(1)}, s32[64]{0:T(128)}, u32[]{:S(2)}) copy-start(s32[64]{0:T(128)} %param.10) | copy-start | bytes 772
  42.8 25.5 %all-to-all-start.2 = ((bf16[16,128,128]{2,1,0:T(8,128)(2,1)}), bf16[16,128,128]{2,1,0:T(8,128)(2,1)S(1)}, u32[]{:S(2)}, u32[]{:S(2)}) async-start(bf16[16,128,128]{2,1,0:T(8,128)(2,1)} %broadcast_in_dim.14), calls=%async_computation.2 | async-start | bytes 1048576 | tf_op jit(solution)/shard_map/all_to_all | solution.py:64
  53.9 23.4 %copy-start.3 = (s32[64]{0:T(128)S(1)}, s32[64]{0:T(128)}, u32[]{:S(2)}) copy-start(s32[64]{0:T(128)} %param.11) | copy-start | bytes 772
  68.3 7.0 %copy-start.2 = (bf16[16,128,128]{2,1,0:T(8,128)(2,1)}, bf16[16,128,128]{2,1,0:T(8,128)(2,1)S(1)}, u32[]{:S(2)}) copy-start(bf16[16,128,128]{2,1,0:T(8,128)(2,1)S(1)} %all-to-all-done.2) | copy-start | bytes 1572868
  70.1 53.4 %all-to-all-start.3 = ((bf16[16,4,128,128]{3,2,1,0:T(8,128)(2,1)}), bf16[16,4,128,128]{3,2,1,0:T(8,128)(2,1)S(1)}, u32[]{:S(2)}, u32[]{:S(2)}) async-start(bf16[16,4,128,128]{3,2,1,0:T(8,128)(2,1)} %broadcast_in_dim.16), calls=%async_computation.3 | async-start | bytes 4194304 | tf_op jit(solution)/shard_map/all_to_all | solution.py:67
  75.2 48.2 %all-gather.3.cloned.1.call-start = ((), (), s32[]{:S(2)}) async-start(), calls=%async_computation.4 | async-start | bytes 2621440 | tf_op jit(solution)/shard_map/all_gather | solution.py:65
  123.4 1.3 copy-start.1
Sparse Core Ops, SparseCore 0:
  78.1 31.5 all-gather.2

commit v9 on v8

--- a/solution.py
+++ b/solution.py
@@ -59,13 +59,15 @@
     own_visible = lax.dynamic_slice_in_dim(visible, own_slot, per_device, 0)
     n_zl, n_x, n_y = lax.axis_size("zl"), lax.axis_size("x"), lax.axis_size("y")
     plane_size = n_zl * n_y
-    keys = both_parts[:, :HD]
     values_t = both_parts[:, HD:].T
-    key_plane = lax.all_to_all(jnp.broadcast_to(keys[None], (plane_size,) + keys.shape), ("zl", "y"), 0, 0)
-    key_all = lax.all_gather(key_plane, "x", axis=0, tiled=True).reshape(-1, HD)
-    value_row = lax.all_gather(values_t[None], "x", axis=0, tiled=True)
+    split = HD // 2
+    part_a = jnp.concatenate([both_parts[:, :HD], values_t[:split]], axis=0)
+    part_b = values_t[split:]
+    plane_a = lax.all_to_all(jnp.broadcast_to(part_a[None], (plane_size,) + part_a.shape), ("zl", "y"), 0, 0)
+    key_all = lax.all_gather(plane_a, "x", axis=0, tiled=True).reshape(-1, HD)
+    row_b = lax.all_gather(part_b[None], "x", axis=0, tiled=True)
     value_all = lax.all_to_all(
-        jnp.broadcast_to(value_row[None], (plane_size,) + value_row.shape), ("zl", "y"), 0, 0
+        jnp.broadcast_to(row_b[None], (plane_size,) + row_b.shape), ("zl", "y"), 0, 0
     ).reshape(-1, HD)
     slots = jnp.arange(visible.shape[1], dtype=jnp.int32)
     slot_zl = slots // (n_x * n_y)
@@ -88,6 +90,8 @@
     rows = tok_rows * head_count
     steps = order_physical.shape[1] // 2
 
+    split = HD // 2
+
     def kernel(order_ref, count_ref, q_ref, ka_ref, kb_ref, va_ref, vb_ref, o_ref, q_scr, m_scr, l_scr, acc_scr):
         i = pl.program_id(0)
 
@@ -101,7 +105,7 @@
             acc_scr[...] = jnp.zeros(acc_scr.shape, jnp.float32)
 
         def scores_of(k_ref, causal):
-            s_t = jnp.dot(k_ref[...], q_scr[...], preferred_element_type=jnp.float32) * score_scale
+            s_t = jnp.dot(k_ref[:BLOCK, :], q_scr[...], preferred_element_type=jnp.float32) * score_scale
             if causal:
                 key = lax.broadcasted_iota(jnp.int32, (BLOCK, rows), 0)
                 tok = lax.broadcasted_iota(jnp.int32, (BLOCK, rows), 1) % tok_rows
@@ -109,22 +113,26 @@
             return s_t
 
         def step(first_causal, with_second):
-            parts = [(scores_of(ka_ref, first_causal), va_ref)]
+            parts = [(scores_of(ka_ref, first_causal), ka_ref, va_ref)]
             if with_second:
-                parts.append((scores_of(kb_ref, False), vb_ref))
+                parts.append((scores_of(kb_ref, False), kb_ref, vb_ref))
             m_old = m_scr[...]
             m_new = m_old
-            for s_t, _ in parts:
+            for s_t, _, _ in parts:
                 m_new = jnp.maximum(m_new, jnp.max(s_t, axis=0, keepdims=True))
             factor = jnp.exp(m_old - m_new)
             l_new = l_scr[...] * factor
-            acc_new = acc_scr[...] * factor
-            for s_t, ref in parts:
+            acc_lo = acc_scr[:split, :] * factor
+            acc_hi = acc_scr[split:, :] * factor
+            for s_t, k_ref, v_ref in parts:
                 expo = jnp.exp(s_t - m_new)
                 l_new = l_new + jnp.sum(expo, axis=0, keepdims=True)
-                acc_new = acc_new + jnp.dot(ref[...], expo.astype(jnp.bfloat16), preferred_element_type=jnp.float32)
+                weights = expo.astype(jnp.bfloat16)
+                acc_lo = acc_lo + jnp.dot(k_ref[BLOCK:, :], weights, preferred_element_type=jnp.float32)
+                acc_hi = acc_hi + jnp.dot(v_ref[...], weights, preferred_element_type=jnp.float32)
             l_scr[...] = l_new
-            acc_scr[...] = acc_new
+            acc_scr[:split, :] = acc_lo
+            acc_scr[split:, :] = acc_hi
             m_scr[...] = m_new
 
         n = count_ref[0]
@@ -158,10 +166,10 @@
         grid=(steps,),
         in_specs=[
             pl.BlockSpec((tok_rows, head_count * HD), lambda i, o, c: (0, 0)),
-            pl.BlockSpec((BLOCK, HD), lambda i, o, c: (o[0, 2 * i], 0)),
-            pl.BlockSpec((BLOCK, HD), lambda i, o, c: (o[0, 2 * i + 1], 0)),
-            pl.BlockSpec((HD, BLOCK), lambda i, o, c: (o[1, 2 * i], 0)),
-            pl.BlockSpec((HD, BLOCK), lambda i, o, c: (o[1, 2 * i + 1], 0)),
+            pl.BlockSpec((BLOCK + split, HD), lambda i, o, c: (o[0, 2 * i], 0)),
+            pl.BlockSpec((BLOCK + split, HD), lambda i, o, c: (o[0, 2 * i + 1], 0)),
+            pl.BlockSpec((HD - split, BLOCK), lambda i, o, c: (o[1, 2 * i], 0)),
+            pl.BlockSpec((HD - split, BLOCK), lambda i, o, c: (o[1, 2 * i + 1], 0)),
         ],
         out_specs=pl.BlockSpec((tok_rows, head_count * HD), lambda i, o, c: (0, 0)),
         scratch_shapes=[

time: 155 us -> 149 us (0.961)
  blocking collectives: 15 us -> 48.1 us
  waiting for transfers between devices: 58.2 us -> 30 us
  starting transfers between devices: 26.6 us -> 14.7 us
  Pallas kernels: 21 us -> 23.2 us
    all_to_all x0 -> x1, blocking collectives: none -> 31.6 us  [shards(): lax.all_to_all(jnp.broadcast_to(part_a[None], (plane_size,) + part_a.shap...]
    all_to_all x2 -> x1, waiting for transfers between devices: 44.3 us -> 16.7 us  [shards(): lax.all_to_all(jnp.broadcast_to(row_b[None], (plane_size,) + row_b.shape)...]
    all_to_all x2 -> x1, starting transfers between devices: 16.2 us -> 4.37 us  [shards(): lax.all_to_all(jnp.broadcast_to(row_b[None], (plane_size,) + row_b.shape)...]
    pallas_call x1, Pallas kernels: 21 us -> 23.2 us  [attention(): pl.pallas_call(kernel, grid_spec=grid_spec, out_shape=jax.ShapeDtypeStruc...]
  transfers between devices with their start and end apart: 4 -> 3, of which waited for: 3 -> 2; matrix products, arithmetic and copies ran while one was open for 5% -> 6% of each run, Pallas kernels for 0% -> 0%
where the time goes in v9:
time: 149 us; the launch traced here: 146 us
  blocking collectives  48.1 us (32%)
  waiting for transfers between devices  30 us (20%)
  Pallas kernels  23.2 us (16%)
  starting transfers between devices  14.7 us (10%)
  between operations  14.3 us (10%)
  local copies, waits for them, and re-layouts  8.03 us (5%)
  matrix products  4.55 us (3%)
  other arithmetic  3.42 us (2%)
    all_to_all x1, blocking collectives, shards(): lax.all_to_all(jnp.broadcast_to(part_a[None], (plane_size,) + part_a.shap...  31.6 us
    pallas_call x1, Pallas kernels, attention(): pl.pallas_call(kernel, grid_spec=grid_spec, out_shape=jax.ShapeDtypeStruc...  23.2 us
    all_to_all x1, waiting for transfers between devices, shards(): lax.all_to_all(jnp.broadcast_to(row_b[None], (plane_size,) + row_b.shape)...  16.7 us
    all_to_all x1, waiting for transfers between devices, shards(): from_chip = lax.all_to_all(core_sums, 'zh', 0, 0)  13.3 us
    all_gather x1, blocking collectives, shards(): row_b = lax.all_gather(part_b[None], 'x', axis=0, tiled=True)  11.9 us
    all_to_all x1, starting transfers between devices, shards(): from_chip = lax.all_to_all(core_sums, 'zh', 0, 0)  10.3 us
    all_to_all x1, blocking collectives, shards(): from_core = lax.all_to_all(partial_sums, 'c', 0, 0)  4.58 us
    all_to_all x1, starting transfers between devices, shards(): lax.all_to_all(jnp.broadcast_to(row_b[None], (plane_size,) + row_b.shape)...  4.37 us
  transfers between devices with their start and end apart: 3, of which 2 were waited for; matrix products, arithmetic and copies ran while one was open for 6% of the time, Pallas kernels for 0%

profile of v9, /device:TPU:6, one launch (start us, length us, event | category | flops | bytes accessed | tf_op | source)
XLA Modules:
  0.0 146.2 jit_solution(3237097375628481201)
XLA Ops:
  6.5 0.9 copy-done
  7.5 2.9 %fusion.14 = f32[128,2048]{1,0:T(8,128)S(1)} fusion(bf16[128,1024]{1,0:T(8,128)(2,1)S(1)} %copy-done, bf16[1024,2048]{1,0:T(8,128)(2,1)} %param.8), kind=kOutput, calls=%fused_computation.53 | convolution fusion | flops 536870912 | bytes 5505024 | tf_op jit(solution)/shard_map/dot_general | solution.py:48
  10.4 0.9 reshape.90
  11.3 0.3 copy.46
  11.6 4.6 %all_to_all.20 = f32[2,4,128,256]{3,1,2,0:T(4,128)S(1)} all-to-all(f32[2,4,128,256]{3,1,2,0:T(4,128)S(1)} %bitcast.46), channel_id=1, replica_groups=mesh['zh'=4,'c'=2,'zl'=2,'x'=4,'y'=8] {'c'}, dimensions={0} | all-to-all | bytes 2097152 | tf_op jit(solution)/shard_map/all_to_all | solution.py:50
  16.1 0.4 reduce_sum.41
  16.6 0.9 copy.39
  17.5 10.3 %all-to-all-start.1 = ((f32[4,128,256]{2,1,0:T(8,128)}), f32[4,128,256]{2,1,0:T(8,128)S(1)}, u32[]{:S(2)}, u32[]{:S(2)}) async-start(f32[4,128,256]{2,1,0:T(8,128)} %copy.39), calls=%async_computation.1 | async-start | bytes 1048576 | tf_op jit(solution)/shard_map/all_to_all | solution.py:52
  27.8 0.8 dynamic_slice.7
  28.5 13.3 %all-to-all-done.1 = f32[4,128,256]{2,1,0:T(8,128)S(1)} async-done(((f32[4,128,256]{2,1,0:T(8,128)}), f32[4,128,256]{2,1,0:T(8,128)S(1)}, u32[]{:S(2)}, u32[]{:S(2)}) %all-to-all-start.1) | async-done | bytes 524320 | tf_op jit(solution)/shard_map/all_to_all | solution.py:52
  42.3 31.6 %all_to_all.21 = bf16[16,192,128]{2,1,0:T(8,128)(2,1)} all-to-all(bf16[16,192,128]{2,1,0:T(8,128)(2,1)S(1)} %broadcast_in_dim.14), channel_id=1, replica_groups=mesh['zh'=4,'c'=2,'zl'=2,'x'=4,'y'=8] {'zl','y'}, dimensions={0} | all-to-all | bytes 1572864 | tf_op jit(solution)/shard_map/all_to_all | solution.py:66
  73.8 0.2 convolution_minimum_fusion.6
  74.1 0.2 convolution_minimum_fusion.5
  74.3 0.2 convolution_minimum_fusion.4
  74.4 0.2 convolution_minimum_fusion.3
  74.7 11.9 %all-gather = bf16[256,128]{1,0:T(8,128)(2,1)S(1)} all-gather(bf16[64,128]{1,0:T(8,128)(2,1)S(1)} %copy.42), channel_id=2, replica_groups=mesh['zh'=4,'c'=2,'zl'=2,'x'=4,'y'=8] {'x'}, dimensions={0}, use_global_device_ids=true | all-gather | bytes 81920 | tf_op jit(solution)/shard_map/all_gather | solution.py:68
  86.6 1.2 broadcast_in_dim.16
  87.9 4.4 %all-to-all-start.3 = ((bf16[16,4,64,128]{3,2,1,0:T(8,128)(2,1)}), bf16[16,4,64,128]{3,2,1,0:T(8,128)(2,1)S(1)}, u32[]{:S(2)}, u32[]{:S(2)}) async-start(bf16[16,4,64,128]{3,2,1,0:T(8,128)(2,1)} %broadcast_in_dim.16), calls=%async_computation.3 | async-start | bytes 2097152 | tf_op jit(solution)/shard_map/all_to_all | solution.py:69
  92.2 0.2 convolution_minimum_fusion.2
  92.4 0.2 convolution_minimum_fusion.1
  92.8 0.2 fusion.4
  93.0 0.2 fusion.3
  93.5 0.6 fusion.10
  94.8 0.7 iota_minimum_fusion
  95.5 0.2 select_reduce_fusion
  95.7 0.7 fusion.11
  96.4 0.8 gather_fusion.1
  97.2 0.8 gather_fusion
  97.9 0.6 pad_add_fusion.order_ref
  98.5 16.7 %all-to-all-done.3 = bf16[16,4,64,128]{3,2,1,0:T(8,128)(2,1)S(1)} async-done(((bf16[16,4,64,128]{3,2,1,0:T(8,128)(2,1)}), bf16[16,4,64,128]{3,2,1,0:T(8,128)(2,1)S(1)}, u32[]{:S(2)}, u32[]{:S(2)}) %all-to-all-start.3) | async-done | bytes 1048608 | tf_op jit(solution)/shard_map/all_to_all | solution.py:69
  115.2 1.0 copy-done.1
  116.2 23.2 %shard_map.64 = bf16[128,1024]{1,0:T(8,128)(2,1)} custom-call(s32[2,64]{1,0:T(2,128)} %pad_add_fusion.order_ref, s32[1]{0:T(128)} %bitcast.7.count_ref, bf16[128,1024]{1,0:T(8,128)(2,1)} %q_ref.1, bf16[12288,128]{1,0:T(8,128)(2,1)} %bitcast.42, bf16[12288,128]{1,0:T(8,128)(2,1)} %bitcast.43, bf16[4096,128]{1,0:T(8,128)(2,1)} %bitcast.44, ...), custom_call_target="tpu_custom_call" | custom-call | tf_op jit(solution)/shard_map/pallas_call | solution.py:182
  (25 shorter events, 1.0 us)
Async XLA Ops:
  6.5 1.0 copy-start
  16.1 57.7 %copy-start.3 = (s32[64]{0:T(128)S(1)}, s32[64]{0:T(128)}, u32[]{:S(2)}) copy-start(s32[64]{0:T(128)} %param.10) | copy-start | bytes 772
  17.5 24.4 %all-to-all-start.1 = ((f32[4,128,256]{2,1,0:T(8,128)}), f32[4,128,256]{2,1,0:T(8,128)S(1)}, u32[]{:S(2)}, u32[]{:S(2)}) async-start(f32[4,128,256]{2,1,0:T(8,128)} %copy.39), calls=%async_computation.1 | async-start | bytes 1048576 | tf_op jit(solution)/shard_map/all_to_all | solution.py:52
  27.8 87.4 %all-gather.3.cloned.1.call-start = ((), (), s32[]{:S(2)}) async-start(), calls=%async_computation.4 | async-start | bytes 3932160 | tf_op jit(solution)/shard_map/all_gather | solution.py:67
  28.5 64.2 %copy-start.2 = (s32[64]{0:T(128)S(1)}, s32[64]{0:T(128)}, u32[]{:S(2)}) copy-start(s32[64]{0:T(128)} %param.11) | copy-start | bytes 772
  87.9 27.3 %all-to-all-start.3 = ((bf16[16,4,64,128]{3,2,1,0:T(8,128)(2,1)}), bf16[16,4,64,128]{3,2,1,0:T(8,128)(2,1)S(1)}, u32[]{:S(2)}, u32[]{:S(2)}) async-start(bf16[16,4,64,128]{3,2,1,0:T(8,128)(2,1)} %broadcast_in_dim.16), calls=%async_computation.3 | async-start | bytes 2097152 | tf_op jit(solution)/shard_map/all_to_all | solution.py:69
  115.2 1.0 copy-start.1
Sparse Core Ops, SparseCore 0:
  74.0 37.3 all-gather.2

commit v10 on v9

--- a/solution.py
+++ b/solution.py
@@ -13,6 +13,7 @@
 BLOCK = 128
 FSDP_AXES = ("zh", "c")
 SEQ_AXES = ("zl", "x", "y")
+SLOTS_PER_STEP = 4
 
 
 def ancestry_table(parents, slot_block):
@@ -88,11 +89,14 @@
 def attention(order_physical, count, queries, key_all, value_all, head_count, score_scale):
     tok_rows = queries.shape[0]
     rows = tok_rows * head_count
-    steps = order_physical.shape[1] // 2
-
+    group = SLOTS_PER_STEP
+    steps = order_physical.shape[1] // group
     split = HD // 2
 
-    def kernel(order_ref, count_ref, q_ref, ka_ref, kb_ref, va_ref, vb_ref, o_ref, q_scr, m_scr, l_scr, acc_scr):
+    def kernel(order_ref, count_ref, q_ref, *refs):
+        k_refs = refs[:group]
+        v_refs = refs[group:2 * group]
+        o_ref, q_scr, m_scr, l_scr, acc_scr = refs[2 * group:]
         i = pl.program_id(0)
 
         @pl.when(i == 0)
@@ -112,10 +116,10 @@
                 s_t = jnp.where(key <= tok, s_t, -1e30)
             return s_t
 
-        def step(first_causal, with_second):
-            parts = [(scores_of(ka_ref, first_causal), ka_ref, va_ref)]
-            if with_second:
-                parts.append((scores_of(kb_ref, False), kb_ref, vb_ref))
+        def step(first_causal, valid):
+            parts = [
+                (scores_of(k_refs[g], first_causal and g == 0), k_refs[g], v_refs[g]) for g in range(valid)
+            ]
             m_old = m_scr[...]
             m_new = m_old
             for s_t, _, _ in parts:
@@ -135,24 +139,15 @@
             acc_scr[split:, :] = acc_hi
             m_scr[...] = m_new
 
-        n = count_ref[0]
-        second = 2 * i + 1 < n
-
-        @pl.when((i == 0) & second)
-        def _():
-            step(True, True)
-
-        @pl.when((i == 0) & jnp.logical_not(second))
-        def _():
-            step(True, False)
-
-        @pl.when((i > 0) & second)
-        def _():
-            step(False, True)
-
-        @pl.when((i > 0) & (2 * i < n) & jnp.logical_not(second))
-        def _():
-            step(False, False)
+        left = count_ref[0] - group * i
+        for first in (True, False):
+            for valid in range(1, group + 1):
+                at_valid = (left >= valid) if valid == group else (left == valid)
+                at_step = (i == 0) if first else (i > 0)
+
+                @pl.when(at_step & at_valid)
+                def _(first=first, valid=valid):
+                    step(first, valid)
 
         @pl.when(i == steps - 1)
         def _():
@@ -161,16 +156,18 @@
                 result = acc_scr[:, cols] / l_scr[:, cols]
                 o_ref[:, h * HD:(h + 1) * HD] = result.T.astype(o_ref.dtype)
 
+    def key_map(g):
+        return lambda i, o, c: (o[0, group * i + g], 0)
+
+    def value_map(g):
+        return lambda i, o, c: (o[1, group * i + g], 0)
+
     grid_spec = pltpu.PrefetchScalarGridSpec(
         num_scalar_prefetch=2,
         grid=(steps,),
-        in_specs=[
-            pl.BlockSpec((tok_rows, head_count * HD), lambda i, o, c: (0, 0)),
-            pl.BlockSpec((BLOCK + split, HD), lambda i, o, c: (o[0, 2 * i], 0)),
-            pl.BlockSpec((BLOCK + split, HD), lambda i, o, c: (o[0, 2 * i + 1], 0)),
-            pl.BlockSpec((HD - split, BLOCK), lambda i, o, c: (o[1, 2 * i], 0)),
-            pl.BlockSpec((HD - split, BLOCK), lambda i, o, c: (o[1, 2 * i + 1], 0)),
-        ],
+        in_specs=[pl.BlockSpec((tok_rows, head_count * HD), lambda i, o, c: (0, 0))]
+        + [pl.BlockSpec((BLOCK + split, HD), key_map(g)) for g in range(group)]
+        + [pl.BlockSpec((HD - split, BLOCK), value_map(g)) for g in range(group)],
         out_specs=pl.BlockSpec((tok_rows, head_count * HD), lambda i, o, c: (0, 0)),
         scratch_shapes=[
             pltpu.VMEM((HD, rows), jnp.bfloat16),
@@ -184,7 +181,7 @@
         grid_spec=grid_spec,
         out_shape=jax.ShapeDtypeStruct((tok_rows, head_count * HD), jnp.bfloat16),
         compiler_params=pltpu.CompilerParams(dimension_semantics=("arbitrary",)),
-    )(order_physical, count, queries, key_all, key_all, value_all, value_all)
+    )(order_physical, count, queries, *([key_all] * group), *([value_all] * group))
 
 
 def solution(mesh):

time: 149 us -> 146 us (0.980); the launches traced: 146 us -> 146 us
  no operation moved by 1% of the time
where the time goes in v10:
time: 146 us
  blocking collectives  48.1 us (33%)
  waiting for transfers between devices  30 us (21%)
  Pallas kernels  22.8 us (16%)
  starting transfers between devices  14.7 us (10%)
  between operations  14.3 us (10%)
  local copies, waits for them, and re-layouts  8.03 us (5%)
  matrix products  4.55 us (3%)
  other arithmetic  3.42 us (2%)
    all_to_all x1, blocking collectives, shards(): lax.all_to_all(jnp.broadcast_to(part_a[None], (plane_size,) + part_a.shap...  31.6 us
    pallas_call x1, Pallas kernels, attention(): pl.pallas_call(kernel, grid_spec=grid_spec, out_shape=jax.ShapeDtypeStruc...  22.8 us
    all_to_all x1, waiting for transfers between devices, shards(): lax.all_to_all(jnp.broadcast_to(row_b[None], (plane_size,) + row_b.shape)...  16.7 us
    all_to_all x1, waiting for transfers between devices, shards(): from_chip = lax.all_to_all(core_sums, 'zh', 0, 0)  13.3 us
    all_gather x1, blocking collectives, shards(): row_b = lax.all_gather(part_b[None], 'x', axis=0, tiled=True)  11.9 us
    all_to_all x1, starting transfers between devices, shards(): from_chip = lax.all_to_all(core_sums, 'zh', 0, 0)  10.3 us
    all_to_all x1, blocking collectives, shards(): from_core = lax.all_to_all(partial_sums, 'c', 0, 0)  4.58 us
    all_to_all x1, starting transfers between devices, shards(): lax.all_to_all(jnp.broadcast_to(row_b[None], (plane_size,) + row_b.shape)...  4.37 us
  transfers between devices with their start and end apart: 3, of which 2 were waited for; matrix products, arithmetic and copies ran while one was open for 6% of the time, Pallas kernels for 0%

profile of v10, /device:TPU:6, one launch (start us, length us, event | category | flops | bytes accessed | tf_op | source)
XLA Modules:
  0.0 145.8 jit_solution(8945592708054633157)
XLA Ops:
  6.5 0.9 copy-done
  7.5 2.9 %fusion.14 = f32[128,2048]{1,0:T(8,128)S(1)} fusion(bf16[128,1024]{1,0:T(8,128)(2,1)S(1)} %copy-done, bf16[1024,2048]{1,0:T(8,128)(2,1)} %param.8), kind=kOutput, calls=%fused_computation.53 | convolution fusion | flops 536870912 | bytes 5505024 | tf_op jit(solution)/shard_map/dot_general | solution.py:49
  10.4 0.9 reshape.90
  11.3 0.3 copy.46
  11.6 4.6 %all_to_all.20 = f32[2,4,128,256]{3,1,2,0:T(4,128)S(1)} all-to-all(f32[2,4,128,256]{3,1,2,0:T(4,128)S(1)} %bitcast.50), channel_id=1, replica_groups=mesh['zh'=4,'c'=2,'zl'=2,'x'=4,'y'=8] {'c'}, dimensions={0} | all-to-all | bytes 2097152 | tf_op jit(solution)/shard_map/all_to_all | solution.py:51
  16.1 0.4 reduce_sum.41
  16.6 0.9 copy.39
  17.5 10.3 %all-to-all-start.1 = ((f32[4,128,256]{2,1,0:T(8,128)}), f32[4,128,256]{2,1,0:T(8,128)S(1)}, u32[]{:S(2)}, u32[]{:S(2)}) async-start(f32[4,128,256]{2,1,0:T(8,128)} %copy.39), calls=%async_computation.1 | async-start | bytes 1048576 | tf_op jit(solution)/shard_map/all_to_all | solution.py:53
  27.8 0.8 dynamic_slice.7
  28.5 13.3 %all-to-all-done.1 = f32[4,128,256]{2,1,0:T(8,128)S(1)} async-done(((f32[4,128,256]{2,1,0:T(8,128)}), f32[4,128,256]{2,1,0:T(8,128)S(1)}, u32[]{:S(2)}, u32[]{:S(2)}) %all-to-all-start.1) | async-done | bytes 524320 | tf_op jit(solution)/shard_map/all_to_all | solution.py:53
  42.3 31.6 %all_to_all.21 = bf16[16,192,128]{2,1,0:T(8,128)(2,1)} all-to-all(bf16[16,192,128]{2,1,0:T(8,128)(2,1)S(1)} %broadcast_in_dim.14), channel_id=1, replica_groups=mesh['zh'=4,'c'=2,'zl'=2,'x'=4,'y'=8] {'zl','y'}, dimensions={0} | all-to-all | bytes 1572864 | tf_op jit(solution)/shard_map/all_to_all | solution.py:67
  73.8 0.2 convolution_minimum_fusion.6
  74.1 0.2 convolution_minimum_fusion.5
  74.3 0.2 convolution_minimum_fusion.4
  74.4 0.2 convolution_minimum_fusion.3
  74.7 11.9 %all-gather = bf16[256,128]{1,0:T(8,128)(2,1)S(1)} all-gather(bf16[64,128]{1,0:T(8,128)(2,1)S(1)} %copy.42), channel_id=2, replica_groups=mesh['zh'=4,'c'=2,'zl'=2,'x'=4,'y'=8] {'x'}, dimensions={0}, use_global_device_ids=true | all-gather | bytes 81920 | tf_op jit(solution)/shard_map/all_gather | solution.py:69
  86.6 1.2 broadcast_in_dim.16
  87.9 4.4 %all-to-all-start.3 = ((bf16[16,4,64,128]{3,2,1,0:T(8,128)(2,1)}), bf16[16,4,64,128]{3,2,1,0:T(8,128)(2,1)S(1)}, u32[]{:S(2)}, u32[]{:S(2)}) async-start(bf16[16,4,64,128]{3,2,1,0:T(8,128)(2,1)} %broadcast_in_dim.16), calls=%async_computation.3 | async-start | bytes 2097152 | tf_op jit(solution)/shard_map/all_to_all | solution.py:70
  92.2 0.2 convolution_minimum_fusion.2
  92.4 0.2 convolution_minimum_fusion.1
  92.8 0.2 fusion.4
  93.0 0.2 fusion.3
  93.5 0.6 fusion.10
  94.8 0.7 iota_minimum_fusion
  95.5 0.2 select_reduce_fusion
  95.7 0.7 fusion.11
  96.4 0.8 gather_fusion.1
  97.2 0.8 gather_fusion
  97.9 0.6 pad_add_fusion.order_ref
  98.5 16.7 %all-to-all-done.3 = bf16[16,4,64,128]{3,2,1,0:T(8,128)(2,1)S(1)} async-done(((bf16[16,4,64,128]{3,2,1,0:T(8,128)(2,1)}), bf16[16,4,64,128]{3,2,1,0:T(8,128)(2,1)S(1)}, u32[]{:S(2)}, u32[]{:S(2)}) %all-to-all-start.3) | async-done | bytes 1048608 | tf_op jit(solution)/shard_map/all_to_all | solution.py:70
  115.2 1.0 copy-done.1
  116.2 22.8 %shard_map.64 = bf16[128,1024]{1,0:T(8,128)(2,1)} custom-call(s32[2,64]{1,0:T(2,128)} %pad_add_fusion.order_ref, s32[1]{0:T(128)} %bitcast.7.count_ref, bf16[128,1024]{1,0:T(8,128)(2,1)} %q_ref.1, bf16[12288,128]{1,0:T(8,128)(2,1)} %bitcast.42, bf16[12288,128]{1,0:T(8,128)(2,1)} %bitcast.43, bf16[12288,128]{1,0:T(8,128)(2,1)} %bitcast.44, ...), custom_call_target="tpu_custom_call" | custom-call | tf_op jit(solution)/shard_map/pallas_call | solution.py:179
  (25 shorter events, 1.0 us)
Async XLA Ops:
  6.5 1.0 copy-start
  16.1 57.7 %copy-start.3 = (s32[64]{0:T(128)S(1)}, s32[64]{0:T(128)}, u32[]{:S(2)}) copy-start(s32[64]{0:T(128)} %param.10) | copy-start | bytes 772
  17.5 24.4 %all-to-all-start.1 = ((f32[4,128,256]{2,1,0:T(8,128)}), f32[4,128,256]{2,1,0:T(8,128)S(1)}, u32[]{:S(2)}, u32[]{:S(2)}) async-start(f32[4,128,256]{2,1,0:T(8,128)} %copy.39), calls=%async_computation.1 | async-start | bytes 1048576 | tf_op jit(solution)/shard_map/all_to_all | solution.py:53
  27.8 87.4 %all-gather.3.cloned.1.call-start = ((), (), s32[]{:S(2)}) async-start(), calls=%async_computation.4 | async-start | bytes 3932160 | tf_op jit(solution)/shard_map/all_gather | solution.py:68
  28.5 64.2 %copy-start.2 = (s32[64]{0:T(128)S(1)}, s32[64]{0:T(128)}, u32[]{:S(2)}) copy-start(s32[64]{0:T(128)} %param.11) | copy-start | bytes 772
  87.9 27.3 %all-to-all-start.3 = ((bf16[16,4,64,128]{3,2,1,0:T(8,128)(2,1)}), bf16[16,4,64,128]{3,2,1,0:T(8,128)(2,1)S(1)}, u32[]{:S(2)}, u32[]{:S(2)}) async-start(bf16[16,4,64,128]{3,2,1,0:T(8,128)(2,1)} %broadcast_in_dim.16), calls=%async_computation.3 | async-start | bytes 2097152 | tf_op jit(solution)/shard_map/all_to_all | solution.py:70
  115.2 1.0 copy-start.1
Sparse Core Ops, SparseCore 0:
  74.0 37.3 all-gather.2

commit v11 on v10

--- a/solution.py
+++ b/solution.py
@@ -13,7 +13,7 @@
 BLOCK = 128
 FSDP_AXES = ("zh", "c")
 SEQ_AXES = ("zl", "x", "y")
-SLOTS_PER_STEP = 4
+SLOTS_PER_STEP = 8
 
 
 def ancestry_table(parents, slot_block):

time: 146 us -> 144 us (0.986)
  the two profiles are of different devices: /device:TPU:6 before, /device:TPU:62 now
where the time goes in v11:
time: 144 us; the launch traced here: 143 us
  blocking collectives  46.8 us (32%)
  waiting for transfers between devices  28.9 us (20%)
  Pallas kernels  21.8 us (15%)
  starting transfers between devices  15.6 us (11%)
  between operations  14.3 us (10%)
  local copies, waits for them, and re-layouts  8.03 us (6%)
  matrix products  4.55 us (3%)
  other arithmetic  3.42 us (2%)
    all_to_all x1, blocking collectives, shards(): lax.all_to_all(jnp.broadcast_to(part_a[None], (plane_size,) + part_a.shap...  30.3 us
    pallas_call x1, Pallas kernels, attention(): pl.pallas_call(kernel, grid_spec=grid_spec, out_shape=jax.ShapeDtypeStruc...  21.8 us
    all_to_all x1, waiting for transfers between devices, shards(): lax.all_to_all(jnp.broadcast_to(row_b[None], (plane_size,) + row_b.shape)...  15.6 us
    all_to_all x1, waiting for transfers between devices, shards(): from_chip = lax.all_to_all(core_sums, 'zh', 0, 0)  13.3 us
    all_gather x1, blocking collectives, shards(): row_b = lax.all_gather(part_b[None], 'x', axis=0, tiled=True)  11.9 us
    all_to_all x1, starting transfers between devices, shards(): from_chip = lax.all_to_all(core_sums, 'zh', 0, 0)  10.3 us
    all_to_all x1, starting transfers between devices, shards(): lax.all_to_all(jnp.broadcast_to(row_b[None], (plane_size,) + row_b.shape)...  5.32 us
    all_to_all x1, blocking collectives, shards(): from_core = lax.all_to_all(partial_sums, 'c', 0, 0)  4.58 us
  transfers between devices with their start and end apart: 3, of which 2 were waited for; matrix products, arithmetic and copies ran while one was open for 6% of the time, Pallas kernels for 0%

profile of v11, /device:TPU:62, one launch (start us, length us, event | category | flops | bytes accessed | tf_op | source)
XLA Modules:
  0.0 143.4 jit_solution(143938978586673274)
XLA Ops:
  6.5 0.9 copy-done
  7.5 2.9 %fusion.14 = f32[128,2048]{1,0:T(8,128)S(1)} fusion(bf16[128,1024]{1,0:T(8,128)(2,1)S(1)} %copy-done, bf16[1024,2048]{1,0:T(8,128)(2,1)} %param.8), kind=kOutput, calls=%fused_computation.53 | convolution fusion | flops 536870912 | bytes 5505024 | tf_op jit(solution)/shard_map/dot_general | solution.py:49
  10.4 0.9 reshape.90
  11.3 0.3 copy.46
  11.6 4.6 %all_to_all.20 = f32[2,4,128,256]{3,1,2,0:T(4,128)S(1)} all-to-all(f32[2,4,128,256]{3,1,2,0:T(4,128)S(1)} %bitcast.58), channel_id=1, replica_groups=mesh['zh'=4,'c'=2,'zl'=2,'x'=4,'y'=8] {'c'}, dimensions={0} | all-to-all | bytes 2097152 | tf_op jit(solution)/shard_map/all_to_all | solution.py:51
  16.1 0.4 reduce_sum.41
  16.6 0.9 copy.39
  17.5 10.3 %all-to-all-start.1 = ((f32[4,128,256]{2,1,0:T(8,128)}), f32[4,128,256]{2,1,0:T(8,128)S(1)}, u32[]{:S(2)}, u32[]{:S(2)}) async-start(f32[4,128,256]{2,1,0:T(8,128)} %copy.39), calls=%async_computation.1 | async-start | bytes 1048576 | tf_op jit(solution)/shard_map/all_to_all | solution.py:53
  27.8 0.8 dynamic_slice.7
  28.5 13.3 %all-to-all-done.1 = f32[4,128,256]{2,1,0:T(8,128)S(1)} async-done(((f32[4,128,256]{2,1,0:T(8,128)}), f32[4,128,256]{2,1,0:T(8,128)S(1)}, u32[]{:S(2)}, u32[]{:S(2)}) %all-to-all-start.1) | async-done | bytes 524320 | tf_op jit(solution)/shard_map/all_to_all | solution.py:53
  42.3 30.3 %all_to_all.21 = bf16[16,192,128]{2,1,0:T(8,128)(2,1)} all-to-all(bf16[16,192,128]{2,1,0:T(8,128)(2,1)S(1)} %broadcast_in_dim.14), channel_id=1, replica_groups=mesh['zh'=4,'c'=2,'zl'=2,'x'=4,'y'=8] {'zl','y'}, dimensions={0} | all-to-all | bytes 1572864 | tf_op jit(solution)/shard_map/all_to_all | solution.py:67
  72.6 0.2 convolution_minimum_fusion.6
  72.8 0.2 convolution_minimum_fusion.5
  73.0 0.2 convolution_minimum_fusion.4
  73.1 0.2 convolution_minimum_fusion.3
  73.4 11.9 %all-gather = bf16[256,128]{1,0:T(8,128)(2,1)S(1)} all-gather(bf16[64,128]{1,0:T(8,128)(2,1)S(1)} %copy.42), channel_id=2, replica_groups=mesh['zh'=4,'c'=2,'zl'=2,'x'=4,'y'=8] {'x'}, dimensions={0}, use_global_device_ids=true | all-gather | bytes 81920 | tf_op jit(solution)/shard_map/all_gather | solution.py:69
  85.3 1.2 broadcast_in_dim.16
  86.6 5.3 %all-to-all-start.3 = ((bf16[16,4,64,128]{3,2,1,0:T(8,128)(2,1)}), bf16[16,4,64,128]{3,2,1,0:T(8,128)(2,1)S(1)}, u32[]{:S(2)}, u32[]{:S(2)}) async-start(bf16[16,4,64,128]{3,2,1,0:T(8,128)(2,1)} %broadcast_in_dim.16), calls=%async_computation.3 | async-start | bytes 2097152 | tf_op jit(solution)/shard_map/all_to_all | solution.py:70
  92.1 0.2 convolution_minimum_fusion.1
  92.2 0.2 convolution_minimum_fusion
  92.4 0.2 fusion.4
  92.6 0.2 fusion.3
  93.2 0.6 fusion.10
  94.5 0.7 iota_minimum_fusion
  95.2 0.2 select_reduce_fusion
  95.4 0.7 fusion.11
  96.0 0.8 gather_fusion.1
  96.8 0.8 gather_fusion
  97.6 0.6 pad_add_fusion.order_ref
  98.2 15.6 %all-to-all-done.3 = bf16[16,4,64,128]{3,2,1,0:T(8,128)(2,1)S(1)} async-done(((bf16[16,4,64,128]{3,2,1,0:T(8,128)(2,1)}), bf16[16,4,64,128]{3,2,1,0:T(8,128)(2,1)S(1)}, u32[]{:S(2)}, u32[]{:S(2)}) %all-to-all-start.3) | async-done | bytes 1048608 | tf_op jit(solution)/shard_map/all_to_all | solution.py:70
  113.8 1.0 copy-done.1
  114.8 21.8 %shard_map.64 = bf16[128,1024]{1,0:T(8,128)(2,1)} custom-call(s32[2,64]{1,0:T(2,128)} %pad_add_fusion.order_ref, s32[1]{0:T(128)} %bitcast.7.count_ref, bf16[128,1024]{1,0:T(8,128)(2,1)} %q_ref.1, bf16[12288,128]{1,0:T(8,128)(2,1)} %bitcast.42, bf16[12288,128]{1,0:T(8,128)(2,1)} %bitcast.43, bf16[12288,128]{1,0:T(8,128)(2,1)} %bitcast.44, ...), custom_call_target="tpu_custom_call" | custom-call | tf_op jit(solution)/shard_map/pallas_call | solution.py:179
  (25 shorter events, 1.0 us)
Async XLA Ops:
  6.5 1.0 copy-start
  16.1 56.4 %copy-start.3 = (s32[64]{0:T(128)S(1)}, s32[64]{0:T(128)}, u32[]{:S(2)}) copy-start(s32[64]{0:T(128)} %param.10) | copy-start | bytes 772
  17.5 24.4 %all-to-all-start.1 = ((f32[4,128,256]{2,1,0:T(8,128)}), f32[4,128,256]{2,1,0:T(8,128)S(1)}, u32[]{:S(2)}, u32[]{:S(2)}) async-start(f32[4,128,256]{2,1,0:T(8,128)} %copy.39), calls=%async_computation.1 | async-start | bytes 1048576 | tf_op jit(solution)/shard_map/all_to_all | solution.py:53
  27.8 86.0 %all-gather.3.cloned.1.call-start = ((), (), s32[]{:S(2)}) async-start(), calls=%async_computation.4 | async-start | bytes 3932160 | tf_op jit(solution)/shard_map/all_gather | solution.py:68
  28.5 63.9 %copy-start.2 = (s32[64]{0:T(128)S(1)}, s32[64]{0:T(128)}, u32[]{:S(2)}) copy-start(s32[64]{0:T(128)} %param.11) | copy-start | bytes 772
  86.6 27.2 %all-to-all-start.3 = ((bf16[16,4,64,128]{3,2,1,0:T(8,128)(2,1)}), bf16[16,4,64,128]{3,2,1,0:T(8,128)(2,1)S(1)}, u32[]{:S(2)}, u32[]{:S(2)}) async-start(bf16[16,4,64,128]{3,2,1,0:T(8,128)(2,1)} %broadcast_in_dim.16), calls=%async_computation.3 | async-start | bytes 2097152 | tf_op jit(solution)/shard_map/all_to_all | solution.py:70
  113.8 1.0 copy-start.1
Sparse Core Ops, SparseCore 0:
  72.7 38.1 all-gather.2
